TPU v7x, 256 devices: a whole 4x4x8 slice. The times are simulated.
256 devices in a mesh: seq: 64 (over y, z, core), pb: 4 (over x).
Axes of the slice: x: 4, y: 4, z: 8, core: 2. Of those that a mesh axis runs over, the one named last changes fastest.
Arguments:
- tokens: bfloat16 [16384, 2048], P('seq'), may hold values from -0.119628906 to 0.119628906
- w_query: bfloat16 [2048, 2048], P(None, 'pb')
- w_key: bfloat16 [2048, 2048], P(None, 'pb')
- w_value: bfloat16 [2048, 2048], P(None, 'pb'), may hold values from -0.125 to 0.125
- w_out: bfloat16 [2048, 2048], P('pb'), may hold values from -0.125 to 0.125
- gain_attn: float32 [2048], replicated, may hold values from 0.1 to 1.9
- gain_embed: float32 [2048], replicated, may hold values from 0.1 to 1.9
- queries: bfloat16 [256, 32, 2048], P(('seq', 'pb')), may hold values from -0.125 to 0.125
- query_lengths: int32 [256], P(('seq', 'pb')), may hold values from 8 to 32
- group_lengths: int32 [128], replicated, may hold values from 1 to 1024, 16384 in all
- teacher: float32 [256, 128], P(('seq', 'pb')), may hold values from -12 to 12
Outputs:
- embedded: bfloat16 [16384, 2048], P('seq')
- scores: float32 [256, 128], P(('seq', 'pb'))
- score_gradient: float32 [256, 128], P(('seq', 'pb'))
- distill_loss: float32 [], replicated
Inputs may be any that keep to these rules, and one draw needn't show every extreme that they name: `group_lengths`: the groups cover the document in order: the lengths sum to 16384.
All inputs are finite; a program needn't handle non-finite values.
Results may differ from a plain program's by a relative error of at most 0.013.
Values may be sent and summed in bfloat16 or wider, within the bound.
No kernel may reach another device: no remote copies, remote signals or barrier semaphores. Data moves between devices by JAX's collectives and lax.ppermute only.
A program may use at most 128 MiB of HBM per device.

v0:
```python
import jax
import jax.numpy as jnp
from jax import lax
from jax.sharding import PartitionSpec as P


HD = 128
WIN = 2048
LQ = 32


EPSILON = 1e-06
SOFTMAX_TEMP = 0.1


def sided_fetch(x, axis, distance):
    count = lax.axis_size(axis)
    pairs = []
    for target in range(count):
        source = target - distance if target % 2 == 0 else target + distance
        if 0 <= source < count:
            pairs.append((source, target))
    return lax.ppermute(x, axis, pairs)


def joint_fetch(x, seq_count, pb_count, source_of):
    pairs = []
    for s in range(seq_count):
        for p in range(pb_count):
            from_s, from_p = source_of(s, p)
            pairs.append((from_s * pb_count + from_p, s * pb_count + p))
    return lax.ppermute(x, ("seq", "pb"), pairs)


def xor_swap(x, axis, bit):
    count = lax.axis_size(axis)
    return lax.ppermute(x, axis, [(i, i ^ bit) for i in range(count)])


def ring_shift(x, axis, by):
    count = lax.axis_size(axis)
    return lax.ppermute(x, axis, [(i, (i + by) % count) for i in range(count)])


HALVING_BITS = (1, 2, 16, 4, 32, 8)


def halving_max(values, axis, steps):
    place = lax.axis_index(axis)
    rows = values.shape[0]
    width = rows.bit_length() - 1
    bits = [b for b in HALVING_BITS if b < rows]
    split = values.reshape((2,) * width + values.shape[1:])
    order = [width - 1 - (b.bit_length() - 1) for b in bits]
    split = jnp.transpose(split, order + list(range(width, split.ndim)))
    values = split.reshape((rows,) + values.shape[1:])
    for bit in bits[:steps]:
        half = values.shape[0] // 2
        mine = ((place & bit) != 0).astype(jnp.int32)
        keep = lax.dynamic_slice_in_dim(values, mine * half, half, 0)
        send = lax.dynamic_slice_in_dim(values, (1 - mine) * half, half, 0)
        values = jnp.maximum(keep, xor_swap(send, axis, bit))
    return values


def butterfly_sum(value, axis, bits=None):
    count = lax.axis_size(axis)
    if bits is None:
        bits = [b for b in HALVING_BITS if b < count]
    for bit in bits:
        value = value + xor_swap(value, axis, bit)
    return value


def rms_scale(values, gain):
    mean_sq = jnp.mean(values * values, axis=-1, keepdims=True)
    return values * lax.rsqrt(mean_sq + EPSILON) * gain


def segmented_max(values, group_id):
    span_len = values.shape[-1]
    stride = 1
    while stride < span_len:
        filler = jnp.full(values.shape[:-1] + (stride,), -jnp.inf, values.dtype)
        shifted = jnp.concatenate([filler, values[..., :-stride]], axis=-1)
        prior_id = jnp.concatenate([jnp.full((stride,), -1, jnp.int32), group_id[:-stride]])
        values = jnp.where((prior_id == group_id)[None, :], jnp.maximum(values, shifted), values)
        stride = stride * 2
    return values


def per_device(
    tokens,
    w_query,
    w_key,
    w_value,
    w_out,
    gain_attn,
    gain_embed,
    queries,
    query_lengths,
    group_lengths,
    teacher,
):
    shard_rows = tokens.shape[0]
    seq_count = lax.axis_size("seq")
    seq_place = lax.axis_index("seq")
    head_width = w_query.shape[1]
    heads_here = head_width // HD
    half_win = WIN // 2
    reach_count = half_win // shard_rows
    my_start = seq_place * shard_rows
    total_tokens = shard_rows * seq_count
    residual = tokens.astype(jnp.float32)
    normed = rms_scale(residual, gain_attn).astype(jnp.bfloat16)
    pb_count = lax.axis_size("pb")
    core = seq_place % 2
    half_rows = w_out.shape[0] // 2
    w_side = joint_fetch(
        w_out, seq_count, pb_count, lambda s, p: (s, (p + 1 - 2 * (s % 2)) % pb_count)
    )
    w_far = joint_fetch(
        lax.dynamic_slice_in_dim(w_out, core * half_rows, half_rows, 0),
        seq_count,
        pb_count,
        lambda s, p: (s, (p + 2) % pb_count),
    )
    w_early = jnp.concatenate([w_out, w_side, w_far], axis=0)
    q_local = jnp.dot(normed, w_query, preferred_element_type=jnp.float32).astype(jnp.bfloat16)
    k_local = jnp.dot(normed, w_key, preferred_element_type=jnp.float32).astype(jnp.bfloat16)
    v_local = jnp.dot(normed, w_value, preferred_element_type=jnp.float32).astype(jnp.bfloat16)
    toward = 2 * core - 1
    k_heads_local = k_local.reshape(shard_rows, heads_here, HD).transpose(1, 0, 2)
    v_heads_local = v_local.reshape(shard_rows, heads_here, HD).transpose(1, 0, 2)
    key_value = jnp.stack([k_heads_local, v_heads_local])
    fetched = [sided_fetch(key_value, "seq", d) for d in range(1, reach_count + 1)]
    handed = lax.ppermute(
        jnp.stack([key_value] + fetched[: reach_count - 1]),
        "seq",
        [(i, i ^ 1) for i in range(seq_count)],
    )
    blocks = [key_value] + fetched + [handed[j] for j in range(reach_count)]
    window = jnp.concatenate(blocks, axis=2)
    span_rows = window.shape[2]
    block_shift = jnp.asarray(
        [0] + list(range(1, reach_count + 1)) + [-d for d in range(1, reach_count + 1)], jnp.int32
    )
    block_start = (seq_place + toward * block_shift) * shard_rows
    q_pos = my_start + jnp.arange(shard_rows, dtype=jnp.int32)
    k_pos = (block_start[:, None] + jnp.arange(shard_rows, dtype=jnp.int32)[None, :]).reshape(span_rows)
    in_window = (
        (jnp.abs(q_pos[:, None] - k_pos[None, :]) <= half_win)
        & (k_pos >= 0)[None, :]
        & (k_pos < total_tokens)[None, :]
    )
    q_heads = q_local.reshape(shard_rows, heads_here, HD).transpose(1, 0, 2)
    k_heads = window[0]
    v_heads = window[1]
    logits = jnp.einsum(
        "hqd,hkd->hqk", q_heads, k_heads, preferred_element_type=jnp.float32
    ) * HD ** (-0.5)
    logits = jnp.where(in_window[None], logits, -jnp.inf)
    row_max = jnp.max(logits, axis=-1, keepdims=True)
    exp_terms = jnp.exp(logits - row_max)
    weights = (exp_terms / jnp.sum(exp_terms, axis=-1, keepdims=True)).astype(jnp.bfloat16)
    w_sib = lax.ppermute(
        jnp.concatenate([w_side, w_far], axis=0), "seq", [(i, i ^ 1) for i in range(seq_count)]
    )
    mixed = jnp.einsum("hqk,hkd->qhd", weights, v_heads, preferred_element_type=jnp.float32)
    mixed = mixed.reshape(shard_rows, head_width).astype(jnp.bfloat16)
    from_prev, from_far, from_next = [ring_shift(mixed, "pb", k) for k in range(1, pb_count)]
    first_core = core == 0
    far_lo, far_hi = from_far[:, :half_rows], from_far[:, half_rows:]
    mixed_early = jnp.concatenate(
        [mixed, jnp.where(first_core, from_next, from_prev), jnp.where(first_core, far_lo, far_hi)],
        axis=1,
    )
    mixed_late = jnp.concatenate(
        [jnp.where(first_core, from_prev, from_next), jnp.where(first_core, far_hi, far_lo)], axis=1
    )
    attn_sum = jnp.dot(mixed_early, w_early, preferred_element_type=jnp.float32) + jnp.dot(
        mixed_late, w_sib, preferred_element_type=jnp.float32
    )
    embedded = rms_scale(residual + attn_sum, gain_embed).astype(jnp.bfloat16)
    group_end = jnp.cumsum(group_lengths)
    group_start = group_end - group_lengths
    group_id = jnp.sum((group_end[None, :] <= q_pos[:, None]).astype(jnp.int32), axis=1)
    last_local = jnp.clip(group_end - 1 - my_start, 0, shard_rows - 1)
    present = (group_start < my_start + shard_rows) & (group_end > my_start)
    q_piece = lax.all_gather(queries, "seq", axis=0, tiled=True)
    count = q_piece.shape[0]
    q_rows = q_piece.reshape(count * q_piece.shape[1], q_piece.shape[2])
    similar = jnp.einsum("td,rd->tr", q_rows, embedded, preferred_element_type=jnp.float32)
    running = segmented_max(similar, group_id)
    picked = jnp.take(running, last_local, axis=1)
    picked = jnp.where(present[None, :], picked, -jnp.inf)
    part_max = picked.reshape(count, q_piece.shape[1], picked.shape[-1])
    own_count = queries.shape[0]
    group_bits = HALVING_BITS[3:]
    token_max = halving_max(part_max, "seq", len(HALVING_BITS) - len(group_bits))
    member = 0
    for bit in group_bits:
        member = member * 2 + ((seq_place & bit) != 0).astype(jnp.int32)
    group_size = 2 ** len(group_bits)
    side_row = jnp.concatenate([teacher, query_lengths.astype(jnp.float32)[:, None]], axis=1)
    side_rows = jnp.where(
        (jnp.arange(group_size, dtype=jnp.int32) == member)[:, None],
        jnp.broadcast_to(side_row, (group_size, side_row.shape[1])),
        -jnp.inf,
    )
    slot_width = token_max.shape[1] * token_max.shape[2]
    packed = jnp.concatenate([token_max.reshape(group_size, slot_width), side_rows], axis=1)
    for bit in group_bits:
        packed = jnp.maximum(packed, xor_swap(packed, "seq", bit))
    token_max = packed[:, :slot_width].reshape(group_size, *part_max.shape[1:])
    side_rows = packed[:, slot_width:]
    group_teacher = side_rows[:, :-1]
    group_lengths_f = side_rows[:, -1]
    live_mask = (
        jnp.arange(LQ, dtype=jnp.int32)[None, :] < group_lengths_f.astype(jnp.int32)[:, None]
    ).astype(jnp.float32)
    group_scores = jnp.sum(token_max * live_mask[:, :, None], axis=1) / group_lengths_f[:, None]
    student_scores = group_scores / SOFTMAX_TEMP
    student_scores = student_scores - jnp.max(student_scores, axis=-1, keepdims=True)
    student_log_prob = student_scores - jnp.log(
        jnp.sum(jnp.exp(student_scores), axis=-1, keepdims=True)
    )
    target_scores = group_teacher / SOFTMAX_TEMP
    target_scores = target_scores - jnp.max(target_scores, axis=-1, keepdims=True)
    log_t = target_scores - jnp.log(jnp.sum(jnp.exp(target_scores), axis=-1, keepdims=True))
    teacher_prob = jnp.exp(log_t)
    kl_terms = jnp.sum(teacher_prob * (log_t - student_log_prob), axis=-1)
    query_count_all = own_count * seq_count * lax.axis_size("pb")
    loss_sum = butterfly_sum(butterfly_sum(jnp.sum(kl_terms), "seq", HALVING_BITS[:3]), "pb")
    distill_loss = loss_sum / query_count_all
    gradient_rows = (jnp.exp(student_log_prob) - teacher_prob) / (SOFTMAX_TEMP * query_count_all)
    scores = lax.dynamic_slice_in_dim(group_scores, member, 1, 0)
    score_gradient = lax.dynamic_slice_in_dim(gradient_rows, member, 1, 0)
    return (embedded, scores, score_gradient, distill_loss)


def solution(mesh):
    placed = (
        P("seq", None),
        P(None, "pb"),
        P(None, "pb"),
        P(None, "pb"),
        P("pb", None),
        P(),
        P(),
        P(("seq", "pb"), None, None),
        P(("seq", "pb")),
        P(),
        P(("seq", "pb"), None),
    )

    return jax.shard_map(
        per_device,
        mesh=mesh,
        in_specs=placed,
        out_specs=(P("seq", None), P(("seq", "pb"), None), P(("seq", "pb"), None), P()),
        check_vma=False,
    )
```

profile of v0, /device:TPU:2, one launch (start us, length us, event | category | flops | bytes accessed | tf_op | source)
XLA Modules:
  0.0 218.3 jit_solution(12274739222475053314)
XLA Ops:
  7.2 0.7 all-gather.2.cloned.1.call-update
  7.9 1.5 fusion.20
  9.5 2.1 fusion.24
  11.7 0.8 fusion.25
  12.6 1.3 fusion.58
  13.9 0.7 collective-permute-start
  14.6 5.1 %collective-permute-start.1 = (bf16[2,4,256,128]{3,2,1,0:T(8,128)(2,1)}, bf16[2,4,256,128]{3,2,1,0:T(8,128)(2,1)S(1)}, u32[]{:S(2)}, u32[]{:S(2)}) collective-permute-start(bf16[2,4,256,128]{3,2,1,0:T(8,128)(2,1)} %get-tuple-element.12), channel_id=1, source_target_pairs={{12,4},{0,8},{20,12},{8,16},{28,20},{16,24},{36,28},{24,32},{44,36... | collective-permute-start | bytes 1572872 | tf_op jit(solution)/shard_map/ppermute | solution.py:23
  19.7 0.7 collective-permute-start.2
  20.4 7.2 %collective-permute-start.3 = (bf16[2,4,256,128]{3,2,1,0:T(8,128)(2,1)}, bf16[2,4,256,128]{3,2,1,0:T(8,128)(2,1)}, u32[]{:S(2)}, u32[]{:S(2)}) collective-permute-start(bf16[2,4,256,128]{3,2,1,0:T(8,128)(2,1)} %get-tuple-element.12), channel_id=1, source_target_pairs={{20,4},{28,12},{0,16},{36,20},{8,24},{44,28},{16,32},{52,36},{24,4... | collective-permute-start | bytes 1572872 | tf_op jit(solution)/shard_map/ppermute | solution.py:23
  27.6 0.5 collective-permute-start.8
  28.6 1.3 constant_dynamic-slice_fusion.5
  30.0 2.5 %collective-permute-start.9 = (bf16[256,2048]{1,0:T(8,128)(2,1)S(1)}, bf16[256,2048]{1,0:T(8,128)(2,1)}, u32[]{:S(2)}, u32[]{:S(2)}) collective-permute-start(bf16[256,2048]{1,0:T(8,128)(2,1)S(1)} %constant_dynamic-slice_fusion.5), channel_id=1, source_target_pairs={{2,0},{3,1},{0,2},{1,3},{6,4},{7,5},{4,6},{5,7},{10,8},{11,9},{8,1... | collective-permute-start | bytes 3145736 | tf_op jit(solution)/shard_map/ppermute | solution.py:32
  32.5 5.2 %collective-permute-done.1 = bf16[2,4,256,128]{3,2,1,0:T(8,128)(2,1)S(1)} collective-permute-done((bf16[2,4,256,128]{3,2,1,0:T(8,128)(2,1)}, bf16[2,4,256,128]{3,2,1,0:T(8,128)(2,1)S(1)}, u32[]{:S(2)}, u32[]{:S(2)}) %collective-permute-start.1) | collective-permute-done | bytes 524320 | tf_op jit(solution)/shard_map/ppermute | solution.py:23
  37.6 1.7 pad_maximum_fusion.1
  39.3 17.8 %collective-permute-start.4 = (bf16[4,2,4,256,128]{4,3,2,1,0:T(8,128)(2,1)}, bf16[4,2,4,256,128]{4,3,2,1,0:T(8,128)(2,1)}, u32[]{:S(2)}, u32[]{:S(2)}) collective-permute-start(bf16[4,2,4,256,128]{4,3,2,1,0:T(8,128)(2,1)} %pad_maximum_fusion.1), channel_id=1, source_target_pairs={{0,4},{4,0},{8,12},{12,8},{16,20},{20,16},{24,28},{28,24},{32,36},... | collective-permute-start | bytes 6291464 | tf_op jit(solution)/shard_map/ppermute | solution.py:137
  57.4 3.4 %fusion.26 = bf16[32,4,8,128]{3,2,1,0:T(8,128)(2,1)} fusion(bf16[2048,512]{1,0:T(8,128)(2,1)} %param.13, bf16[256,2048]{1,0:T(8,128)(2,1)} %param.12, f32[2048]{0:T(1024)S(1)} %copy-done.17, f32[256]{0:T(256)S(1)} %add_rsqrt_fusion.1), kind=kOutput, calls=%fused_computation.48 | convolution fusion | flops 539099136 | bytes 3417088 | tf_op jit(solution)/shard_map/dot_general | solution.py:129
  60.8 1.7 fusion.19
  62.5 14.9 %collective-permute-done.9 = bf16[256,2048]{1,0:T(8,128)(2,1)} collective-permute-done((bf16[256,2048]{1,0:T(8,128)(2,1)S(1)}, bf16[256,2048]{1,0:T(8,128)(2,1)}, u32[]{:S(2)}, u32[]{:S(2)}) %collective-permute-start.9) | collective-permute-done | bytes 1048608 | tf_op jit(solution)/shard_map/ppermute | solution.py:32
  77.3 2.2 %pad_maximum_fusion = bf16[768,2048]{1,0:T(8,128)(2,1)S(1)} fusion(bf16[256,2048]{1,0:T(8,128)(2,1)} %collective-permute-done.9, bf16[512,2048]{1,0:T(8,128)(2,1)} %collective-permute-done.8), kind=kLoop, calls=%fused_computation.16 | loop fusion | flops 6291456 | bytes 6291456 | tf_op jit(solution)/shard_map/concatenate | solution.py:167
  79.9 0.9 constant_dynamic-update-slice_fusion.3
  80.8 0.9 constant_dynamic-update-slice_fusion.2
  81.7 0.9 constant_dynamic-update-slice_fusion.1
  82.6 2.0 constant_dynamic-update-slice_fusion
  84.6 2.0 fusion.35
  86.6 1.9 fusion.34
  88.5 2.1 fusion.33
  90.6 1.9 fusion.32
  92.5 5.1 %fusion.62 = f32[4,256]{1,0:T(4,128)S(1)} fusion(pred[256,2304]{1,0:T(8,128)(4,1)} %fusion.19, bf16[2,4,2304,128]{3,2,1,0:T(8,128)(2,1)} %fusion.32, bf16[32,4,8,128]{3,2,1,0:T(8,128)(2,1)S(1)} %copy-done.18), kind=kOutput, calls=%fused_computation.143 | convolution fusion | flops 613419264 | bytes 3215360 | tf_op jit(solution)/shard_map/sub | solution.py:164
  97.6 7.6 %fusion.23 = bf16[4,128,256]{2,1,0:T(8,128)(2,1)} fusion(f32[4,256]{1,0:T(4,128)S(1)} %fusion.62, bf16[2,4,2304,128]{3,2,1,0:T(8,128)(2,1)} %fusion.32, pred[256,2304]{1,0:T(8,128)(4,1)} %fusion.19, bf16[32,4,8,128]{3,2,1,0:T(8,128)(2,1)S(1)} %copy-done.18), kind=kOutput, calls=%fused_computation.42 | convolution fusion | flops 1219890432 | bytes 5836800 | tf_op jit(solution)/shard_map/hqk,hkd->qhd/dot_general | solution.py:169
  105.1 2.4 %collective-permute-start.7 = (bf16[256,512]{0,1:T(8,128)(2,1)}, bf16[256,512]{0,1:T(8,128)(2,1)S(1)}, u32[]{:S(2)}, u32[]{:S(2)}) collective-permute-start(bf16[256,512]{0,1:T(8,128)(2,1)} %bitcast.148), channel_id=1, source_target_pairs={{0,2},{1,3},{2,0},{3,1},{4,6},{5,7},{6,4},{7,5},{8,10},{9,11},{10,... | collective-permute-start | bytes 786440 | tf_op jit(solution)/shard_map/ppermute | solution.py:42
  107.7 2.0 collective-permute-start.6
  109.7 6.4 %collective-permute-done.7 = bf16[256,512]{0,1:T(8,128)(2,1)S(1)} collective-permute-done((bf16[256,512]{0,1:T(8,128)(2,1)}, bf16[256,512]{0,1:T(8,128)(2,1)S(1)}, u32[]{:S(2)}, u32[]{:S(2)}) %collective-permute-start.7) | collective-permute-done | bytes 262176 | tf_op jit(solution)/shard_map/ppermute | solution.py:42
  116.1 5.2 %collective-permute-done.5 = bf16[256,512]{0,1:T(8,128)(2,1)} collective-permute-done((bf16[256,512]{0,1:T(8,128)(2,1)}, bf16[256,512]{0,1:T(8,128)(2,1)}, u32[]{:S(2)}, u32[]{:S(2)}) %collective-permute-start.5) | collective-permute-done | bytes 262176 | tf_op jit(solution)/shard_map/ppermute | solution.py:42
  121.3 1.1 broadcast_select_fusion.1
  122.4 3.0 %fusion.36 = f32[256,2048]{1,0:T(8,128)S(1)} fusion(bf16[768,2048]{1,0:T(8,128)(2,1)} %collective-permute-done.10, bf16[256,256]{0,1:T(8,128)(2,1)S(1)} %get-tuple-element.14, bf16[256,512]{0,1:T(8,128)(2,1)S(1)} %get-tuple-element.9), kind=kOutput, calls=%fused_computation.65 | convolution fusion | flops 806092800 | bytes 5636096 | tf_op jit(solution)/shard_map/dot_general | solution.py:181
  125.4 3.7 %multiply_reduce_fusion = (f32[256]{0:T(256)S(1)}, f32[256,2048]{1,0:T(8,128)S(1)}) fusion(f32[256,2048]{1,0:T(8,128)S(1)} %fusion.36, bf16[256,2048]{1,0:T(8,128)(2,1)} %collective-permute-done.9, bf16[512,2048]{1,0:T(8,128)(2,1)} %collective-permute-done.8, bf16[512,2048]{1,0:T(8,128)(2,1)} %param.16, bf16[256,256]{0,1:T(8,128)(2,1)S(1)} %get-tuple-element.13, ...), kind=kOutput, calls=%fused_computation.41 | convolution fusion | flops 1362493184 | bytes 11142144 | tf_op jit(solution)/shard_map/dot_general | solution.py:181
  129.5 6.1 %convolution_bitcast_fusion = f32[2048,256]{0,1:T(8,128)S(1)} fusion(bf16[256,2048]{1,0:T(8,128)(2,1)S(1)} %multiply_convert_fusion, bf16[2048,2048]{1,0:T(8,128)(2,1)} %bitcast.147), kind=kOutput, calls=%fused_computation.28 | convolution fusion | flops 2147483648 | bytes 11534336 | tf_op jit(solution)/shard_map/td,rd->tr/dot_general | solution.py:193
  139.1 1.0 gather_fusion
  140.9 2.0 collective-permute-done.11
  142.9 2.1 dynamic-slice_maximum_fusion
  145.0 1.0 constant_dynamic-slice_fusion.3
  145.9 3.2 %collective-permute-start.12 = (f32[16,32,128]{2,1,0:T(8,128)S(1)}, f32[16,32,128]{2,1,0:T(8,128)S(1)}, u32[]{:S(2)}, u32[]{:S(2)}) collective-permute-start(f32[16,32,128]{2,1,0:T(8,128)S(1)} %constant_dynamic-slice_fusion.3), channel_id=1, source_target_pairs={{0,8},{4,12},{8,0},{12,4},{16,24},{20,28},{24,16},{28,20},{32,40},... | collective-permute-start | bytes 786440 | tf_op jit(solution)/shard_map/ppermute | solution.py:37
  149.8 5.9 %collective-permute-done.12 = f32[16,32,128]{2,1,0:T(8,128)S(1)} collective-permute-done((f32[16,32,128]{2,1,0:T(8,128)S(1)}, f32[16,32,128]{2,1,0:T(8,128)S(1)}, u32[]{:S(2)}, u32[]{:S(2)}) %collective-permute-start.12) | collective-permute-done | bytes 262176 | tf_op jit(solution)/shard_map/ppermute | solution.py:37
  155.8 1.0 dynamic-slice_maximum_fusion.1
  156.8 2.2 %collective-permute-start.13 = (f32[8,32,128]{2,1,0:T(8,128)S(1)}, f32[8,32,128]{2,1,0:T(8,128)S(1)}, u32[]{:S(2)}, u32[]{:S(2)}) collective-permute-start(f32[8,32,128]{2,1,0:T(8,128)S(1)} %constant_dynamic-slice_fusion.2), channel_id=1, source_target_pairs={{0,64},{4,68},{8,72},{12,76},{16,80},{20,84},{24,88},{28,92},{32,9... | collective-permute-start | bytes 393224 | tf_op jit(solution)/shard_map/ppermute | solution.py:37
  159.1 2.9 %collective-permute-done.13 = f32[8,32,128]{2,1,0:T(8,128)S(1)} collective-permute-done((f32[8,32,128]{2,1,0:T(8,128)S(1)}, f32[8,32,128]{2,1,0:T(8,128)S(1)}, u32[]{:S(2)}, u32[]{:S(2)}) %collective-permute-start.13) | collective-permute-done | bytes 131104 | tf_op jit(solution)/shard_map/ppermute | solution.py:37
  162.1 3.0 %collective-permute-start.14 = (f32[8,4225]{1,0:T(8,128)S(1)}, f32[8,4225]{1,0:T(8,128)S(1)}, u32[]{:S(2)}, u32[]{:S(2)}) collective-permute-start(f32[8,4225]{1,0:T(8,128)S(1)} %pad_maximum_fusion.3), channel_id=1, source_target_pairs={{0,16},{4,20},{8,24},{12,28},{16,0},{20,4},{24,8},{28,12},{32,48},... | collective-permute-start | bytes 405608 | tf_op jit(solution)/shard_map/ppermute | solution.py:37
  165.1 5.2 %collective-permute-done.14 = f32[8,4225]{1,0:T(8,128)S(1)} collective-permute-done((f32[8,4225]{1,0:T(8,128)S(1)}, f32[8,4225]{1,0:T(8,128)S(1)}, u32[]{:S(2)}, u32[]{:S(2)}) %collective-permute-start.14) | collective-permute-done | bytes 135232 | tf_op jit(solution)/shard_map/ppermute | solution.py:37
  170.3 3.3 %collective-permute-start.15 = (f32[8,4225]{1,0:T(8,128)S(1)}, f32[8,4225]{1,0:T(8,128)S(1)}, u32[]{:S(2)}, u32[]{:S(2)}) collective-permute-start(f32[8,4225]{1,0:T(8,128)S(1)} %fusion.57), channel_id=1, source_target_pairs={{0,128},{4,132},{8,136},{12,140},{16,144},{20,148},{24,152},{28,15... | collective-permute-start | bytes 405608 | tf_op jit(solution)/shard_map/ppermute | solution.py:37
  173.6 3.4 %collective-permute-done.15 = f32[8,4225]{1,0:T(8,128)S(1)} collective-permute-done((f32[8,4225]{1,0:T(8,128)S(1)}, f32[8,4225]{1,0:T(8,128)S(1)}, u32[]{:S(2)}, u32[]{:S(2)}) %collective-permute-start.15) | collective-permute-done | bytes 135232 | tf_op jit(solution)/shard_map/ppermute | solution.py:37
  177.0 5.0 %collective-permute-start.16 = (f32[8,4225]{1,0:T(8,128)S(1)}, f32[8,4225]{1,0:T(8,128)S(1)}, u32[]{:S(2)}, u32[]{:S(2)}) collective-permute-start(f32[8,4225]{1,0:T(8,128)S(1)} %max.64), channel_id=1, source_target_pairs={{0,32},{4,36},{8,40},{12,44},{16,48},{20,52},{24,56},{28,60},{32,0... | collective-permute-start | bytes 405608 | tf_op jit(solution)/shard_map/ppermute | solution.py:37
  182.0 4.3 %collective-permute-done.16 = f32[8,4225]{1,0:T(8,128)S(1)} collective-permute-done((f32[8,4225]{1,0:T(8,128)S(1)}, f32[8,4225]{1,0:T(8,128)S(1)}, u32[]{:S(2)}, u32[]{:S(2)}) %collective-permute-start.16) | collective-permute-done | bytes 135232 | tf_op jit(solution)/shard_map/ppermute | solution.py:37
  187.4 0.7 multiply_reduce_fusion.1
  188.1 0.5 constant_dynamic-slice_fusion.1
  188.6 0.5 constant_dynamic-slice_fusion
  189.1 0.4 collective-permute-done.17
  190.8 3.6 %collective-permute-start.18 = (f32[]{:T(128)}, f32[]{:T(128)}, u32[]{:S(2)}, u32[]{:S(2)}) collective-permute-start(f32[]{:T(128)} %add.199), channel_id=1, source_target_pairs={{0,8},{4,12},{8,0},{12,4},{16,24},{20,28},{24,16},{28,20},{32,40},... | collective-permute-start | bytes 20 | tf_op jit(solution)/shard_map/ppermute | solution.py:37
  194.4 0.4 collective-permute-done.18
  195.4 3.0 %collective-permute-start.19 = (f32[]{:T(128)}, f32[]{:T(128)}, u32[]{:S(2)}, u32[]{:S(2)}) collective-permute-start(f32[]{:T(128)} %add.200), channel_id=1, source_target_pairs={{0,64},{4,68},{8,72},{12,76},{16,80},{20,84},{24,88},{28,92},{32,9... | collective-permute-start | bytes 20 | tf_op jit(solution)/shard_map/ppermute | solution.py:37
  198.4 0.8 collective-permute-done.19
  199.7 3.7 %collective-permute-start.20 = (f32[]{:T(128)}, f32[]{:T(128)}, u32[]{:S(2)}, u32[]{:S(2)}) collective-permute-start(f32[]{:T(128)} %add.201), channel_id=1, source_target_pairs={{0,1},{1,0},{2,3},{3,2},{4,5},{5,4},{6,7},{7,6},{8,9},{9,8},{10,11... | collective-permute-start | bytes 20 | tf_op jit(solution)/shard_map/ppermute | solution.py:37
  203.4 0.4 collective-permute-done.20
  204.4 4.9 %collective-permute-start.21 = (f32[]{:T(128)}, f32[]{:T(128)}, u32[]{:S(2)}, u32[]{:S(2)}) collective-permute-start(f32[]{:T(128)} %add.202), channel_id=1, source_target_pairs={{0,2},{1,3},{2,0},{3,1},{4,6},{5,7},{6,4},{7,5},{8,10},{9,11},{10,... | collective-permute-start | bytes 20 | tf_op jit(solution)/shard_map/ppermute | solution.py:37
  209.3 0.4 collective-permute-done.21
  (106 shorter events, 7.2 us)
Async XLA Ops:
  7.2 2.3 %copy-start = (bf16[2048,512]{1,0:T(8,128)(2,1)S(1)}, bf16[2048,512]{1,0:T(8,128)(2,1)}, u32[]{:S(2)}) copy-start(bf16[2048,512]{1,0:T(8,128)(2,1)} %param.14) | copy-start | bytes 6291460
  7.2 122.3 %all-gather.2.cloned.1.call-start = ((), (), s32[]{:S(2)}) async-start(), calls=%async_computation | async-start | bytes 8519680 | tf_op jit(solution)/shard_map/all_gather | solution.py:190
  9.4 2.2 copy-start.8
  9.5 2.2 %copy-start.15 = (bf16[2048,512]{1,0:T(8,128)(2,1)S(1)}, bf16[2048,512]{1,0:T(8,128)(2,1)}, u32[]{:S(2)}) copy-start(bf16[2048,512]{1,0:T(8,128)(2,1)} %param.15) | copy-start | bytes 6291460
  9.5 2.2 %copy-start.17 = (f32[2048]{0:T(1024)S(1)}, f32[2048]{0:T(1024)}, u32[]{:S(2)}) copy-start(f32[2048]{0:T(1024)} %param.17) | copy-start | bytes 24580
  12.5 15.7 %copy-start.12 = (s32[128]{0:T(128)S(1)}, s32[128]{0:T(128)}, u32[]{:S(2)}) copy-start(s32[128]{0:T(128)} %param.21) | copy-start | bytes 1540
  12.5 16.0 %copy-start.14 = (s32[9]{0:T(128)S(1)}, s32[9]{0:T(128)}, u32[]{:S(2)}) copy-start(s32[9]{0:T(128)} %constant.113.clone) | copy-start | bytes 112
  13.9 16.0 %collective-permute-start = (bf16[2,4,256,128]{3,2,1,0:T(8,128)(2,1)}, bf16[2,4,256,128]{3,2,1,0:T(8,128)(2,1)S(1)}, u32[]{:S(2)}, u32[]{:S(2)}) collective-permute-start(bf16[2,4,256,128]{3,2,1,0:T(8,128)(2,1)} %get-tuple-element.12), channel_id=1, source_target_pairs={{8,4},{4,8},{16,12},{12,16},{24,20},{20,24},{32,28},{28,32},{40,36... | collective-permute-start | bytes 1572872 | tf_op jit(solution)/shard_map/ppermute | solution.py:23
  14.6 23.0 %collective-permute-start.1 = (bf16[2,4,256,128]{3,2,1,0:T(8,128)(2,1)}, bf16[2,4,256,128]{3,2,1,0:T(8,128)(2,1)S(1)}, u32[]{:S(2)}, u32[]{:S(2)}) collective-permute-start(bf16[2,4,256,128]{3,2,1,0:T(8,128)(2,1)} %get-tuple-element.12), channel_id=1, source_target_pairs={{12,4},{0,8},{20,12},{8,16},{28,20},{16,24},{36,28},{24,32},{44,36... | collective-permute-start | bytes 1572872 | tf_op jit(solution)/shard_map/ppermute | solution.py:23
  19.7 17.9 %collective-permute-start.2 = (bf16[2,4,256,128]{3,2,1,0:T(8,128)(2,1)}, bf16[2,4,256,128]{3,2,1,0:T(8,128)(2,1)S(1)}, u32[]{:S(2)}, u32[]{:S(2)}) collective-permute-start(bf16[2,4,256,128]{3,2,1,0:T(8,128)(2,1)} %get-tuple-element.12), channel_id=1, source_target_pairs={{16,4},{24,12},{4,16},{32,20},{12,24},{40,28},{20,32},{48,36},{28,... | collective-permute-start | bytes 1572872 | tf_op jit(solution)/shard_map/ppermute | solution.py:23
  20.4 62.2 %collective-permute-start.3 = (bf16[2,4,256,128]{3,2,1,0:T(8,128)(2,1)}, bf16[2,4,256,128]{3,2,1,0:T(8,128)(2,1)}, u32[]{:S(2)}, u32[]{:S(2)}) collective-permute-start(bf16[2,4,256,128]{3,2,1,0:T(8,128)(2,1)} %get-tuple-element.12), channel_id=1, source_target_pairs={{20,4},{28,12},{0,16},{36,20},{8,24},{44,28},{16,32},{52,36},{24,4... | collective-permute-start | bytes 1572872 | tf_op jit(solution)/shard_map/ppermute | solution.py:23
  27.6 49.7 %collective-permute-start.8 = (bf16[512,2048]{1,0:T(8,128)(2,1)}, bf16[512,2048]{1,0:T(8,128)(2,1)}, u32[]{:S(2)}, u32[]{:S(2)}) collective-permute-start(bf16[512,2048]{1,0:T(8,128)(2,1)} %param.16), channel_id=1, source_target_pairs={{1,0},{2,1},{3,2},{0,3},{7,4},{4,5},{5,6},{6,7},{9,8},{10,9},{11,1... | collective-permute-start | bytes 6291464 | tf_op jit(solution)/shard_map/ppermute | solution.py:32
  30.0 9.4 %copy-start.2 = (bf16[2,4,256,128]{3,2,1,0:T(8,128)(2,1)}, bf16[2,4,256,128]{3,2,1,0:T(8,128)(2,1)S(1)}, u32[]{:S(2)}) copy-start(bf16[2,4,256,128]{3,2,1,0:T(8,128)(2,1)S(1)} %collective-permute-done) | copy-start | bytes 1572868
  30.0 47.4 %collective-permute-start.9 = (bf16[256,2048]{1,0:T(8,128)(2,1)S(1)}, bf16[256,2048]{1,0:T(8,128)(2,1)}, u32[]{:S(2)}, u32[]{:S(2)}) collective-permute-start(bf16[256,2048]{1,0:T(8,128)(2,1)S(1)} %constant_dynamic-slice_fusion.5), channel_id=1, source_target_pairs={{2,0},{3,1},{0,2},{1,3},{6,4},{7,5},{4,6},{5,7},{10,8},{11,9},{8,1... | collective-permute-start | bytes 3145736 | tf_op jit(solution)/shard_map/ppermute | solution.py:32
  37.6 1.7 copy-start.4
  37.6 1.7 copy-start.6
  39.3 45.3 %collective-permute-start.4 = (bf16[4,2,4,256,128]{4,3,2,1,0:T(8,128)(2,1)}, bf16[4,2,4,256,128]{4,3,2,1,0:T(8,128)(2,1)}, u32[]{:S(2)}, u32[]{:S(2)}) collective-permute-start(bf16[4,2,4,256,128]{4,3,2,1,0:T(8,128)(2,1)} %pad_maximum_fusion.1), channel_id=1, source_target_pairs={{0,4},{4,0},{8,12},{12,8},{16,20},{20,16},{24,28},{28,24},{32,36},... | collective-permute-start | bytes 6291464 | tf_op jit(solution)/shard_map/ppermute | solution.py:137
  62.5 17.4 %copy-start.3 = (bf16[2,4,256,128]{3,2,1,0:T(8,128)(2,1)S(1)}, bf16[2,4,256,128]{3,2,1,0:T(8,128)(2,1)}, u32[]{:S(2)}) copy-start(bf16[2,4,256,128]{3,2,1,0:T(8,128)(2,1)} %copy-done.2) | copy-start | bytes 1572868
  62.5 18.3 %copy-start.5 = (bf16[2,4,256,128]{3,2,1,0:T(8,128)(2,1)S(1)}, bf16[2,4,256,128]{3,2,1,0:T(8,128)(2,1)}, u32[]{:S(2)}) copy-start(bf16[2,4,256,128]{3,2,1,0:T(8,128)(2,1)} %copy-done.4) | copy-start | bytes 1572868
  79.6 2.1 copy-start.7
  79.6 42.8 %collective-permute-start.10 = (bf16[768,2048]{1,0:T(8,128)(2,1)S(1)}, bf16[768,2048]{1,0:T(8,128)(2,1)}, u32[]{:S(2)}, u32[]{:S(2)}) collective-permute-start(bf16[768,2048]{1,0:T(8,128)(2,1)S(1)} %pad_maximum_fusion), channel_id=1, source_target_pairs={{0,4},{4,0},{8,12},{12,8},{16,20},{20,16},{24,28},{28,24},{32,36},... | collective-permute-start | bytes 9437192 | tf_op jit(solution)/shard_map/ppermute | solution.py:166
  84.6 8.0 %copy-start.18 = (bf16[32,4,8,128]{3,2,1,0:T(8,128)(2,1)S(1)}, bf16[32,4,8,128]{3,2,1,0:T(8,128)(2,1)}, u32[]{:S(2)}) copy-start(bf16[32,4,8,128]{3,2,1,0:T(8,128)(2,1)} %fusion.26) | copy-start | bytes 786436
  105.1 10.9 %collective-permute-start.7 = (bf16[256,512]{0,1:T(8,128)(2,1)}, bf16[256,512]{0,1:T(8,128)(2,1)S(1)}, u32[]{:S(2)}, u32[]{:S(2)}) collective-permute-start(bf16[256,512]{0,1:T(8,128)(2,1)} %bitcast.148), channel_id=1, source_target_pairs={{0,2},{1,3},{2,0},{3,1},{4,6},{5,7},{6,4},{7,5},{8,10},{9,11},{10,... | collective-permute-start | bytes 786440 | tf_op jit(solution)/shard_map/ppermute | solution.py:42
  107.6 13.7 %collective-permute-start.5 = (bf16[256,512]{0,1:T(8,128)(2,1)}, bf16[256,512]{0,1:T(8,128)(2,1)}, u32[]{:S(2)}, u32[]{:S(2)}) collective-permute-start(bf16[256,512]{0,1:T(8,128)(2,1)} %bitcast.149), channel_id=1, source_target_pairs={{0,3},{1,0},{2,1},{3,2},{4,7},{5,4},{6,5},{7,6},{8,11},{9,8},{10,9... | collective-permute-start | bytes 786440 | tf_op jit(solution)/shard_map/ppermute | solution.py:42
  107.7 13.6 %collective-permute-start.6 = (bf16[256,512]{0,1:T(8,128)(2,1)}, bf16[256,512]{0,1:T(8,128)(2,1)}, u32[]{:S(2)}, u32[]{:S(2)}) collective-permute-start(bf16[256,512]{0,1:T(8,128)(2,1)} %bitcast.150), channel_id=1, source_target_pairs={{0,1},{1,2},{2,3},{3,0},{4,5},{5,6},{6,7},{7,4},{8,9},{9,10},{10,1... | collective-permute-start | bytes 786440 | tf_op jit(solution)/shard_map/ppermute | solution.py:42
  122.4 3.0 %copy-start.9 = (bf16[256,2048]{1,0:T(8,128)(2,1)S(1)}, bf16[256,2048]{1,0:T(8,128)(2,1)}, u32[]{:S(2)}) copy-start(bf16[256,2048]{1,0:T(8,128)(2,1)} %param.12) | copy-start | bytes 3145732
  122.4 3.0 %copy-start.16 = (bf16[4,128,256]{2,1,0:T(8,128)(2,1)S(1)}, bf16[4,128,256]{2,1,0:T(8,128)(2,1)}, u32[]{:S(2)}) copy-start(bf16[4,128,256]{2,1,0:T(8,128)(2,1)} %fusion.23) | copy-start | bytes 786436
  125.4 3.8 %copy-start.11 = (f32[2048]{0:T(1024)S(1)}, f32[2048]{0:T(1024)}, u32[]{:S(2)}) copy-start(f32[2048]{0:T(1024)} %param.18) | copy-start | bytes 24580
  129.5 6.2 %copy-start.10 = (bf16[256,2048]{1,0:T(8,128)(2,1)}, bf16[256,2048]{1,0:T(8,128)(2,1)S(1)}, u32[]{:S(2)}) copy-start(bf16[256,2048]{1,0:T(8,128)(2,1)S(1)} %multiply_convert_fusion) | copy-start | bytes 3145732
  140.7 9.1 %copy-start.13 = (f32[1,128]{1,0:T(1,128)S(1)}, f32[1,128]{1,0:T(1,128)}, u32[]{:S(2)}) copy-start(f32[1,128]{1,0:T(1,128)} %param.22) | copy-start | bytes 1540
  140.8 2.1 collective-permute-start.11
  142.9 67.4 %copy-start.1 = (bf16[2048,512]{1,0:T(8,128)(2,1)S(1)}, bf16[2048,512]{1,0:T(8,128)(2,1)}, u32[]{:S(2)}) copy-start(bf16[2048,512]{1,0:T(8,128)(2,1)} %param.14) | copy-start | bytes 6291460
  145.9 9.8 %collective-permute-start.12 = (f32[16,32,128]{2,1,0:T(8,128)S(1)}, f32[16,32,128]{2,1,0:T(8,128)S(1)}, u32[]{:S(2)}, u32[]{:S(2)}) collective-permute-start(f32[16,32,128]{2,1,0:T(8,128)S(1)} %constant_dynamic-slice_fusion.3), channel_id=1, source_target_pairs={{0,8},{4,12},{8,0},{12,4},{16,24},{20,28},{24,16},{28,20},{32,40},... | collective-permute-start | bytes 786440 | tf_op jit(solution)/shard_map/ppermute | solution.py:37
  156.8 5.2 %collective-permute-start.13 = (f32[8,32,128]{2,1,0:T(8,128)S(1)}, f32[8,32,128]{2,1,0:T(8,128)S(1)}, u32[]{:S(2)}, u32[]{:S(2)}) collective-permute-start(f32[8,32,128]{2,1,0:T(8,128)S(1)} %constant_dynamic-slice_fusion.2), channel_id=1, source_target_pairs={{0,64},{4,68},{8,72},{12,76},{16,80},{20,84},{24,88},{28,92},{32,9... | collective-permute-start | bytes 393224 | tf_op jit(solution)/shard_map/ppermute | solution.py:37
  162.1 8.2 %collective-permute-start.14 = (f32[8,4225]{1,0:T(8,128)S(1)}, f32[8,4225]{1,0:T(8,128)S(1)}, u32[]{:S(2)}, u32[]{:S(2)}) collective-permute-start(f32[8,4225]{1,0:T(8,128)S(1)} %pad_maximum_fusion.3), channel_id=1, source_target_pairs={{0,16},{4,20},{8,24},{12,28},{16,0},{20,4},{24,8},{28,12},{32,48},... | collective-permute-start | bytes 405608 | tf_op jit(solution)/shard_map/ppermute | solution.py:37
  170.3 6.6 %collective-permute-start.15 = (f32[8,4225]{1,0:T(8,128)S(1)}, f32[8,4225]{1,0:T(8,128)S(1)}, u32[]{:S(2)}, u32[]{:S(2)}) collective-permute-start(f32[8,4225]{1,0:T(8,128)S(1)} %fusion.57), channel_id=1, source_target_pairs={{0,128},{4,132},{8,136},{12,140},{16,144},{20,148},{24,152},{28,15... | collective-permute-start | bytes 405608 | tf_op jit(solution)/shard_map/ppermute | solution.py:37
  177.0 9.3 %collective-permute-start.16 = (f32[8,4225]{1,0:T(8,128)S(1)}, f32[8,4225]{1,0:T(8,128)S(1)}, u32[]{:S(2)}, u32[]{:S(2)}) collective-permute-start(f32[8,4225]{1,0:T(8,128)S(1)} %max.64), channel_id=1, source_target_pairs={{0,32},{4,36},{8,40},{12,44},{16,48},{20,52},{24,56},{28,60},{32,0... | collective-permute-start | bytes 405608 | tf_op jit(solution)/shard_map/ppermute | solution.py:37
  188.1 1.4 collective-permute-start.17
  190.8 4.0 %collective-permute-start.18 = (f32[]{:T(128)}, f32[]{:T(128)}, u32[]{:S(2)}, u32[]{:S(2)}) collective-permute-start(f32[]{:T(128)} %add.199), channel_id=1, source_target_pairs={{0,8},{4,12},{8,0},{12,4},{16,24},{20,28},{24,16},{28,20},{32,40},... | collective-permute-start | bytes 20 | tf_op jit(solution)/shard_map/ppermute | solution.py:37
  195.4 3.8 %collective-permute-start.19 = (f32[]{:T(128)}, f32[]{:T(128)}, u32[]{:S(2)}, u32[]{:S(2)}) collective-permute-start(f32[]{:T(128)} %add.200), channel_id=1, source_target_pairs={{0,64},{4,68},{8,72},{12,76},{16,80},{20,84},{24,88},{28,92},{32,9... | collective-permute-start | bytes 20 | tf_op jit(solution)/shard_map/ppermute | solution.py:37
  199.7 4.0 %collective-permute-start.20 = (f32[]{:T(128)}, f32[]{:T(128)}, u32[]{:S(2)}, u32[]{:S(2)}) collective-permute-start(f32[]{:T(128)} %add.201), channel_id=1, source_target_pairs={{0,1},{1,0},{2,3},{3,2},{4,5},{5,4},{6,7},{7,6},{8,9},{9,8},{10,11... | collective-permute-start | bytes 20 | tf_op jit(solution)/shard_map/ppermute | solution.py:37
  204.4 5.3 %collective-permute-start.21 = (f32[]{:T(128)}, f32[]{:T(128)}, u32[]{:S(2)}, u32[]{:S(2)}) collective-permute-start(f32[]{:T(128)} %add.202), channel_id=1, source_target_pairs={{0,2},{1,3},{2,0},{3,1},{4,6},{5,7},{6,4},{7,5},{8,10},{9,11},{10,... | collective-permute-start | bytes 20 | tf_op jit(solution)/shard_map/ppermute | solution.py:37
Sparse Core Ops, SparseCore 0:
  10.8 95.6 all-gather.1
where the time goes:
time: 221 us; the launch traced here: 218 us
  starting transfers between devices  71.3 us (32%)
  waiting for transfers between devices  58.3 us (26%)
  matrix products  31.7 us (14%)
  between operations  20.2 us (9%)
  local copies, waits for them, and re-layouts  18.8 us (9%)
  other arithmetic  18 us (8%)
    ppermute x11, starting transfers between devices, xor_swap(): return lax.ppermute(x, axis, [(i, i ^ bit) for i in range(count)])  32 us
    ppermute x11, waiting for transfers between devices, xor_swap(): return lax.ppermute(x, axis, [(i, i ^ bit) for i in range(count)])  26 us
    ppermute x1, starting transfers between devices, per_device(): lax.ppermute(jnp.stack([key_value] + fetched[:reach_count - 1]), 'seq', [...  17.8 us
    ppermute x2, waiting for transfers between devices, joint_fetch(): return lax.ppermute(x, ('seq', 'pb'), pairs)  14.9 us
    ppermute x4, starting transfers between devices, sided_fetch(): return lax.ppermute(x, axis, pairs)  13.6 us
    ppermute x3, waiting for transfers between devices, ring_shift(): return lax.ppermute(x, axis, [(i, (i + by) % count) for i in range(count)])  11.6 us
    unnamed x46, local copies, waits for them, and re-layouts  10.9 us
    dot_general x1, matrix products, per_device(): jnp.einsum('hqk,hkd->qhd', weights, v_heads, preferred_element_type=jnp.f...  7.55 us
  transfers between devices with their start and end apart: 23, of which 15 were waited for; matrix products, arithmetic and copies ran while one was open for 23% of the time, Pallas kernels for 0%

commit v1 on v0

--- a/solution.py
+++ b/solution.py
@@ -21,15 +21,6 @@
         if 0 <= source < count:
             pairs.append((source, target))
     return lax.ppermute(x, axis, pairs)
-
-
-def joint_fetch(x, seq_count, pb_count, source_of):
-    pairs = []
-    for s in range(seq_count):
-        for p in range(pb_count):
-            from_s, from_p = source_of(s, p)
-            pairs.append((from_s * pb_count + from_p, s * pb_count + p))
-    return lax.ppermute(x, ("seq", "pb"), pairs)
 
 
 def xor_swap(x, axis, bit):
@@ -114,21 +105,11 @@
     residual = tokens.astype(jnp.float32)
     normed = rms_scale(residual, gain_attn).astype(jnp.bfloat16)
     pb_count = lax.axis_size("pb")
-    core = seq_place % 2
-    half_rows = w_out.shape[0] // 2
-    w_side = joint_fetch(
-        w_out, seq_count, pb_count, lambda s, p: (s, (p + 1 - 2 * (s % 2)) % pb_count)
-    )
-    w_far = joint_fetch(
-        lax.dynamic_slice_in_dim(w_out, core * half_rows, half_rows, 0),
-        seq_count,
-        pb_count,
-        lambda s, p: (s, (p + 2) % pb_count),
-    )
-    w_early = jnp.concatenate([w_out, w_side, w_far], axis=0)
+    w_out_parts = [w_out] + [ring_shift(w_out, "pb", k) for k in range(1, pb_count)]
     q_local = jnp.dot(normed, w_query, preferred_element_type=jnp.float32).astype(jnp.bfloat16)
     k_local = jnp.dot(normed, w_key, preferred_element_type=jnp.float32).astype(jnp.bfloat16)
     v_local = jnp.dot(normed, w_value, preferred_element_type=jnp.float32).astype(jnp.bfloat16)
+    core = seq_place % 2
     toward = 2 * core - 1
     k_heads_local = k_local.reshape(shard_rows, heads_here, HD).transpose(1, 0, 2)
     v_heads_local = v_local.reshape(shard_rows, heads_here, HD).transpose(1, 0, 2)
@@ -163,23 +144,13 @@
     row_max = jnp.max(logits, axis=-1, keepdims=True)
     exp_terms = jnp.exp(logits - row_max)
     weights = (exp_terms / jnp.sum(exp_terms, axis=-1, keepdims=True)).astype(jnp.bfloat16)
-    w_sib = lax.ppermute(
-        jnp.concatenate([w_side, w_far], axis=0), "seq", [(i, i ^ 1) for i in range(seq_count)]
-    )
     mixed = jnp.einsum("hqk,hkd->qhd", weights, v_heads, preferred_element_type=jnp.float32)
     mixed = mixed.reshape(shard_rows, head_width).astype(jnp.bfloat16)
-    from_prev, from_far, from_next = [ring_shift(mixed, "pb", k) for k in range(1, pb_count)]
-    first_core = core == 0
-    far_lo, far_hi = from_far[:, :half_rows], from_far[:, half_rows:]
-    mixed_early = jnp.concatenate(
-        [mixed, jnp.where(first_core, from_next, from_prev), jnp.where(first_core, far_lo, far_hi)],
-        axis=1,
-    )
-    mixed_late = jnp.concatenate(
-        [jnp.where(first_core, from_prev, from_next), jnp.where(first_core, far_hi, far_lo)], axis=1
-    )
-    attn_sum = jnp.dot(mixed_early, w_early, preferred_element_type=jnp.float32) + jnp.dot(
-        mixed_late, w_sib, preferred_element_type=jnp.float32
+    mixed_parts = [mixed] + [ring_shift(mixed, "pb", k) for k in range(1, pb_count)]
+    attn_sum = jnp.dot(
+        jnp.concatenate(mixed_parts, axis=1),
+        jnp.concatenate(w_out_parts, axis=0),
+        preferred_element_type=jnp.float32,
     )
     embedded = rms_scale(residual + attn_sum, gain_embed).astype(jnp.bfloat16)
     group_end = jnp.cumsum(group_lengths)

time: 221 us -> 232 us (1.050)
  starting transfers between devices: 71.3 us -> 108 us
  waiting for transfers between devices: 58.3 us -> 44 us
  local copies, waits for them, and re-layouts: 18.8 us -> 13.8 us
  other arithmetic: 18 us -> 14.7 us
  matrix products: 31.7 us -> 28.8 us
    ppermute x3 -> x6, starting transfers between devices: 4.51 us -> 48.2 us  [ring_shift(): return lax.ppermute(x, axis, [(i, (i + by) % count) for i in range(count)])]
    ppermute x3 -> x0, waiting for transfers between devices: 14.9 us -> none  [the longest x2 14.9 us: joint_fetch(): return lax.ppermute(x, ('seq', 'pb'), pairs)]
    ppermute x3 -> x6, waiting for transfers between devices: 11.6 us -> 4.61 us  [ring_shift(): return lax.ppermute(x, axis, [(i, (i + by) % count) for i in range(count)])]
    ppermute x11, waiting for transfers between devices: 26 us -> 31.2 us  [xor_swap(): return lax.ppermute(x, axis, [(i, i ^ bit) for i in range(count)])]
    ppermute x3 -> x0, starting transfers between devices: 3.31 us -> none  [the longest x2 3.04 us: joint_fetch(): return lax.ppermute(x, ('seq', 'pb'), pairs)]
    unnamed x46 -> x36, local copies, waits for them, and re-layouts: 10.9 us -> 8.35 us
    ppermute x1, starting transfers between devices: 17.8 us -> 15.3 us  [per_device(): lax.ppermute(jnp.stack([key_value] + fetched[:reach_count - 1]), 'seq', [...]
    ppermute x4, waiting for transfers between devices: 5.17 us -> 7.5 us  [sided_fetch(): return lax.ppermute(x, axis, pairs)]
  transfers between devices with their start and end apart: 23 -> 23, of which waited for: 15 -> 14; matrix products, arithmetic and copies ran while one was open for 23% -> 17% of each run, Pallas kernels for 0% -> 0%
where the time goes in v1:
time: 232 us; the launch traced here: 229 us
  starting transfers between devices  108 us (47%)
  waiting for transfers between devices  44 us (19%)
  matrix products  28.8 us (12%)
  between operations  20.5 us (9%)
  other arithmetic  14.7 us (6%)
  local copies, waits for them, and re-layouts  13.8 us (6%)
    ppermute x6, starting transfers between devices, ring_shift(): return lax.ppermute(x, axis, [(i, (i + by) % count) for i in range(count)])  48.2 us
    ppermute x11, waiting for transfers between devices, xor_swap(): return lax.ppermute(x, axis, [(i, i ^ bit) for i in range(count)])  31.2 us
    ppermute x11, starting transfers between devices, xor_swap(): return lax.ppermute(x, axis, [(i, i ^ bit) for i in range(count)])  30.5 us
    ppermute x1, starting transfers between devices, per_device(): lax.ppermute(jnp.stack([key_value] + fetched[:reach_count - 1]), 'seq', [...  15.3 us
    ppermute x4, starting transfers between devices, sided_fetch(): return lax.ppermute(x, axis, pairs)  13.6 us
    unnamed x36, local copies, waits for them, and re-layouts  8.35 us
    ppermute x4, waiting for transfers between devices, sided_fetch(): return lax.ppermute(x, axis, pairs)  7.5 us
    dot_general x1, matrix products, per_device(): jnp.einsum('hqk,hkd->qhd', weights, v_heads, preferred_element_type=jnp.f...  7.26 us
  transfers between devices with their start and end apart: 23, of which 14 were waited for; matrix products, arithmetic and copies ran while one was open for 17% of the time, Pallas kernels for 0%

profile of v1, /device:TPU:2, one launch (start us, length us, event | category | flops | bytes accessed | tf_op | source)
XLA Modules:
  0.0 229.4 jit_solution(12901234713065028111)
XLA Ops:
  7.2 0.7 all-gather.2.cloned.1.call-update
  7.9 1.5 fusion.19
  9.5 2.1 fusion.23
  11.7 0.8 fusion.24
  12.6 1.4 fusion.54
  14.0 0.7 collective-permute-start
  14.7 5.1 %collective-permute-start.1 = (bf16[2,4,256,128]{3,2,1,0:T(8,128)(2,1)}, bf16[2,4,256,128]{3,2,1,0:T(8,128)(2,1)S(1)}, u32[]{:S(2)}, u32[]{:S(2)}) collective-permute-start(bf16[2,4,256,128]{3,2,1,0:T(8,128)(2,1)} %get-tuple-element.10), channel_id=1, source_target_pairs={{12,4},{0,8},{20,12},{8,16},{28,20},{16,24},{36,28},{24,32},{44,36... | collective-permute-start | bytes 1572872 | tf_op jit(solution)/shard_map/ppermute | solution.py:23
  19.8 0.7 collective-permute-start.2
  20.5 7.2 %collective-permute-start.3 = (bf16[2,4,256,128]{3,2,1,0:T(8,128)(2,1)}, bf16[2,4,256,128]{3,2,1,0:T(8,128)(2,1)}, u32[]{:S(2)}, u32[]{:S(2)}) collective-permute-start(bf16[2,4,256,128]{3,2,1,0:T(8,128)(2,1)} %get-tuple-element.10), channel_id=1, source_target_pairs={{20,4},{28,12},{0,16},{36,20},{8,24},{44,28},{16,32},{52,36},{24,4... | collective-permute-start | bytes 1572872 | tf_op jit(solution)/shard_map/ppermute | solution.py:23
  27.7 0.5 collective-permute-start.10
  28.7 1.5 collective-permute-start.8
  30.2 7.5 %collective-permute-done.1 = bf16[2,4,256,128]{3,2,1,0:T(8,128)(2,1)S(1)} collective-permute-done((bf16[2,4,256,128]{3,2,1,0:T(8,128)(2,1)}, bf16[2,4,256,128]{3,2,1,0:T(8,128)(2,1)S(1)}, u32[]{:S(2)}, u32[]{:S(2)}) %collective-permute-start.1) | collective-permute-done | bytes 524320 | tf_op jit(solution)/shard_map/ppermute | solution.py:23
  37.7 2.1 collective-permute-start.9
  39.8 0.8 copy-done.2
  40.7 1.6 pad_maximum_fusion
  42.2 15.3 %collective-permute-start.4 = (bf16[4,2,4,256,128]{4,3,2,1,0:T(8,128)(2,1)}, bf16[4,2,4,256,128]{4,3,2,1,0:T(8,128)(2,1)S(1)}, u32[]{:S(2)}, u32[]{:S(2)}) collective-permute-start(bf16[4,2,4,256,128]{4,3,2,1,0:T(8,128)(2,1)} %pad_maximum_fusion), channel_id=1, source_target_pairs={{0,4},{4,0},{8,12},{12,8},{16,20},{20,16},{24,28},{28,24},{32,36},... | collective-permute-start | bytes 6291464 | tf_op jit(solution)/shard_map/ppermute | solution.py:118
  57.5 2.7 %fusion.25 = bf16[32,4,8,128]{3,2,1,0:T(8,128)(2,1)S(1)} fusion(bf16[2048,512]{1,0:T(8,128)(2,1)} %param.13, bf16[256,2048]{1,0:T(8,128)(2,1)} %param.12, f32[2048]{0:T(1024)S(1)} %copy-done.13, f32[256]{0:T(256)S(1)} %add_rsqrt_fusion.1), kind=kOutput, calls=%fused_computation.48 | convolution fusion | flops 539099136 | bytes 3417088 | tf_op jit(solution)/shard_map/dot_general | solution.py:109
  60.2 1.7 fusion.18
  62.1 0.9 constant_dynamic-update-slice_fusion.3
  63.0 0.9 constant_dynamic-update-slice_fusion.2
  63.9 0.9 constant_dynamic-update-slice_fusion.1
  64.8 1.9 constant_dynamic-update-slice_fusion
  66.7 0.9 fusion.36
  67.6 0.9 fusion.35
  68.5 0.9 fusion.34
  69.4 0.9 fusion.33
  70.3 4.9 %fusion.58 = f32[4,256]{1,0:T(4,128)S(1)} fusion(pred[256,2304]{1,0:T(8,128)(4,1)S(1)} %copy-done.7, bf16[2,4,2304,128]{3,2,1,0:T(8,128)(2,1)} %fusion.33, bf16[32,4,8,128]{3,2,1,0:T(8,128)(2,1)S(1)} %fusion.25), kind=kOutput, calls=%fused_computation.135 | convolution fusion | flops 613419264 | bytes 3215360 | tf_op jit(solution)/shard_map/sub | solution.py:145
  75.2 7.3 %fusion.22 = bf16[4,128,256]{2,1,0:T(8,128)(2,1)S(1)} fusion(f32[4,256]{1,0:T(4,128)S(1)} %fusion.58, bf16[2,4,2304,128]{3,2,1,0:T(8,128)(2,1)} %fusion.33, pred[256,2304]{1,0:T(8,128)(4,1)S(1)} %copy-done.7, bf16[32,4,8,128]{3,2,1,0:T(8,128)(2,1)S(1)} %fusion.25), kind=kOutput, calls=%fused_computation.42 | convolution fusion | flops 1219890432 | bytes 5836800 | tf_op jit(solution)/shard_map/hqk,hkd->qhd/dot_general | solution.py:147
  82.5 1.7 collective-permute-start.5
  84.1 1.3 collective-permute-start.6
  85.4 41.1 %collective-permute-start.7 = (bf16[256,512]{0,1:T(8,128)(2,1)S(1)}, bf16[256,512]{0,1:T(8,128)(2,1)S(1)}, u32[]{:S(2)}, u32[]{:S(2)}) collective-permute-start(bf16[256,512]{0,1:T(8,128)(2,1)S(1)} %bitcast.149), channel_id=1, source_target_pairs={{0,3},{1,0},{2,1},{3,2},{4,7},{5,4},{6,5},{7,6},{8,11},{9,8},{10,9... | collective-permute-start | bytes 786440 | tf_op jit(solution)/shard_map/ppermute | solution.py:33
  126.7 2.1 collective-permute-done.5
  128.8 2.5 %collective-permute-done.7 = bf16[256,512]{0,1:T(8,128)(2,1)S(1)} collective-permute-done((bf16[256,512]{0,1:T(8,128)(2,1)S(1)}, bf16[256,512]{0,1:T(8,128)(2,1)S(1)}, u32[]{:S(2)}, u32[]{:S(2)}) %collective-permute-start.7) | collective-permute-done | bytes 262176 | tf_op jit(solution)/shard_map/ppermute | solution.py:33
  131.3 4.9 %multiply_reduce_fusion = (f32[256]{0:T(256)S(1)}, f32[256,2048]{1,0:T(8,128)S(1)}) fusion(bf16[512,2048]{1,0:T(8,128)(2,1)} %collective-permute-done.10, bf16[512,2048]{1,0:T(8,128)(2,1)} %collective-permute-done.9, bf16[512,2048]{1,0:T(8,128)(2,1)} %collective-permute-done.8, bf16[512,2048]{1,0:T(8,128)(2,1)} %param.16, ...), kind=kOutput, calls=%fused_computation.41 | convolution fusion | flops 2187329280 | bytes 12583936 | tf_op jit(solution)/shard_map/dot_general | solution.py:150
  136.5 6.1 %convolution_bitcast_fusion = f32[2048,256]{0,1:T(8,128)S(1)} fusion(bf16[256,2048]{1,0:T(8,128)(2,1)S(1)} %multiply_convert_fusion, bf16[2048,2048]{1,0:T(8,128)(2,1)} %bitcast.146), kind=kOutput, calls=%fused_computation.29 | convolution fusion | flops 2147483648 | bytes 11534336 | tf_op jit(solution)/shard_map/td,rd->tr/dot_general | solution.py:164
  142.7 0.3 maximum_select_fusion.7
  143.0 0.4 maximum_select_fusion.6
  143.4 0.4 maximum_select_fusion.5
  146.2 1.0 gather_fusion
  147.1 0.3 copy.40
  147.9 2.0 collective-permute-done.11
  150.0 2.1 dynamic-slice_maximum_fusion
  152.0 1.0 constant_dynamic-slice_fusion.3
  153.0 3.2 %collective-permute-start.12 = (f32[16,32,128]{2,1,0:T(8,128)S(1)}, f32[16,32,128]{2,1,0:T(8,128)S(1)}, u32[]{:S(2)}, u32[]{:S(2)}) collective-permute-start(f32[16,32,128]{2,1,0:T(8,128)S(1)} %constant_dynamic-slice_fusion.3), channel_id=1, source_target_pairs={{0,8},{4,12},{8,0},{12,4},{16,24},{20,28},{24,16},{28,20},{32,40},... | collective-permute-start | bytes 786440 | tf_op jit(solution)/shard_map/ppermute | solution.py:28
  156.9 5.9 %collective-permute-done.12 = f32[16,32,128]{2,1,0:T(8,128)S(1)} collective-permute-done((f32[16,32,128]{2,1,0:T(8,128)S(1)}, f32[16,32,128]{2,1,0:T(8,128)S(1)}, u32[]{:S(2)}, u32[]{:S(2)}) %collective-permute-start.12) | collective-permute-done | bytes 262176 | tf_op jit(solution)/shard_map/ppermute | solution.py:28
  162.8 1.0 dynamic-slice_maximum_fusion.1
  163.8 4.4 %collective-permute-start.13 = (f32[8,32,128]{2,1,0:T(8,128)S(1)}, f32[8,32,128]{2,1,0:T(8,128)S(1)}, u32[]{:S(2)}, u32[]{:S(2)}) collective-permute-start(f32[8,32,128]{2,1,0:T(8,128)S(1)} %constant_dynamic-slice_fusion.2), channel_id=1, source_target_pairs={{0,64},{4,68},{8,72},{12,76},{16,80},{20,84},{24,88},{28,92},{32,9... | collective-permute-start | bytes 393224 | tf_op jit(solution)/shard_map/ppermute | solution.py:28
  168.3 2.9 %collective-permute-done.13 = f32[8,32,128]{2,1,0:T(8,128)S(1)} collective-permute-done((f32[8,32,128]{2,1,0:T(8,128)S(1)}, f32[8,32,128]{2,1,0:T(8,128)S(1)}, u32[]{:S(2)}, u32[]{:S(2)}) %collective-permute-start.13) | collective-permute-done | bytes 131104 | tf_op jit(solution)/shard_map/ppermute | solution.py:28
  171.3 1.1 collective-permute-start.14
  172.4 6.9 %collective-permute-done.14 = f32[8,4225]{1,0:T(8,128)S(1)} collective-permute-done((f32[8,4225]{1,0:T(8,128)S(1)}, f32[8,4225]{1,0:T(8,128)S(1)}, u32[]{:S(2)}, u32[]{:S(2)}) %collective-permute-start.14) | collective-permute-done | bytes 135232 | tf_op jit(solution)/shard_map/ppermute | solution.py:28
  179.3 3.4 %collective-permute-start.15 = (f32[8,4225]{1,0:T(8,128)S(1)}, f32[8,4225]{1,0:T(8,128)S(1)}, u32[]{:S(2)}, u32[]{:S(2)}) collective-permute-start(f32[8,4225]{1,0:T(8,128)S(1)} %fusion.53), channel_id=1, source_target_pairs={{0,128},{4,132},{8,136},{12,140},{16,144},{20,148},{24,152},{28,15... | collective-permute-start | bytes 405608 | tf_op jit(solution)/shard_map/ppermute | solution.py:28
  182.7 3.2 %collective-permute-done.15 = f32[8,4225]{1,0:T(8,128)S(1)} collective-permute-done((f32[8,4225]{1,0:T(8,128)S(1)}, f32[8,4225]{1,0:T(8,128)S(1)}, u32[]{:S(2)}, u32[]{:S(2)}) %collective-permute-start.15) | collective-permute-done | bytes 135232 | tf_op jit(solution)/shard_map/ppermute | solution.py:28
  186.0 4.1 %collective-permute-start.16 = (f32[8,4225]{1,0:T(8,128)S(1)}, f32[8,4225]{1,0:T(8,128)S(1)}, u32[]{:S(2)}, u32[]{:S(2)}) collective-permute-start(f32[8,4225]{1,0:T(8,128)S(1)} %max.64), channel_id=1, source_target_pairs={{0,32},{4,36},{8,40},{12,44},{16,48},{20,52},{24,56},{28,60},{32,0... | collective-permute-start | bytes 405608 | tf_op jit(solution)/shard_map/ppermute | solution.py:28
  190.0 5.1 %collective-permute-done.16 = f32[8,4225]{1,0:T(8,128)S(1)} collective-permute-done((f32[8,4225]{1,0:T(8,128)S(1)}, f32[8,4225]{1,0:T(8,128)S(1)}, u32[]{:S(2)}, u32[]{:S(2)}) %collective-permute-start.16) | collective-permute-done | bytes 135232 | tf_op jit(solution)/shard_map/ppermute | solution.py:28
  196.2 0.7 multiply_reduce_fusion.1
  196.9 0.5 constant_dynamic-slice_fusion.1
  197.4 0.5 constant_dynamic-slice_fusion
  199.5 1.4 collective-permute-start.18
  200.9 2.2 collective-permute-done.18
  203.8 3.2 %collective-permute-start.19 = (f32[]{:T(128)}, f32[]{:T(128)}, u32[]{:S(2)}, u32[]{:S(2)}) collective-permute-start(f32[]{:T(128)} %add.192), channel_id=1, source_target_pairs={{0,64},{4,68},{8,72},{12,76},{16,80},{20,84},{24,88},{28,92},{32,9... | collective-permute-start | bytes 20 | tf_op jit(solution)/shard_map/ppermute | solution.py:28
  207.0 0.4 collective-permute-done.19
  208.1 6.6 %collective-permute-start.20 = (f32[]{:T(128)}, f32[]{:T(128)}, u32[]{:S(2)}, u32[]{:S(2)}) collective-permute-start(f32[]{:T(128)} %add.193), channel_id=1, source_target_pairs={{0,1},{1,0},{2,3},{3,2},{4,5},{5,4},{6,7},{7,6},{8,9},{9,8},{10,11... | collective-permute-start | bytes 20 | tf_op jit(solution)/shard_map/ppermute | solution.py:28
  215.6 3.0 %collective-permute-start.21 = (f32[]{:T(128)}, f32[]{:T(128)}, u32[]{:S(2)}, u32[]{:S(2)}) collective-permute-start(f32[]{:T(128)} %add.194), channel_id=1, source_target_pairs={{0,2},{1,3},{2,0},{3,1},{4,6},{5,7},{6,4},{7,5},{8,10},{9,11},{10,... | collective-permute-start | bytes 20 | tf_op jit(solution)/shard_map/ppermute | solution.py:28
  218.7 2.1 collective-permute-done.21
  (91 shorter events, 5.9 us)
Async XLA Ops:
  7.2 2.3 copy-start
  7.2 129.4 %all-gather.2.cloned.1.call-start = ((), (), s32[]{:S(2)}) async-start(), calls=%async_computation | async-start | bytes 8519680 | tf_op jit(solution)/shard_map/all_gather | solution.py:161
  9.4 2.2 copy-start.4
  9.5 2.2 copy-start.12
  9.5 2.2 copy-start.13
  12.5 15.8 %copy-start.9 = (s32[128]{0:T(128)S(1)}, s32[128]{0:T(128)}, u32[]{:S(2)}) copy-start(s32[128]{0:T(128)} %param.21) | copy-start | bytes 1540
  12.5 16.1 %copy-start.11 = (s32[9]{0:T(128)S(1)}, s32[9]{0:T(128)}, u32[]{:S(2)}) copy-start(s32[9]{0:T(128)} %constant.111.clone) | copy-start | bytes 112
  14.0 14.7 %collective-permute-start = (bf16[2,4,256,128]{3,2,1,0:T(8,128)(2,1)}, bf16[2,4,256,128]{3,2,1,0:T(8,128)(2,1)S(1)}, u32[]{:S(2)}, u32[]{:S(2)}) collective-permute-start(bf16[2,4,256,128]{3,2,1,0:T(8,128)(2,1)} %get-tuple-element.10), channel_id=1, source_target_pairs={{8,4},{4,8},{16,12},{12,16},{24,20},{20,24},{32,28},{28,32},{40,36... | collective-permute-start | bytes 1572872 | tf_op jit(solution)/shard_map/ppermute | solution.py:23
  14.7 23.0 %collective-permute-start.1 = (bf16[2,4,256,128]{3,2,1,0:T(8,128)(2,1)}, bf16[2,4,256,128]{3,2,1,0:T(8,128)(2,1)S(1)}, u32[]{:S(2)}, u32[]{:S(2)}) collective-permute-start(bf16[2,4,256,128]{3,2,1,0:T(8,128)(2,1)} %get-tuple-element.10), channel_id=1, source_target_pairs={{12,4},{0,8},{20,12},{8,16},{28,20},{16,24},{36,28},{24,32},{44,36... | collective-permute-start | bytes 1572872 | tf_op jit(solution)/shard_map/ppermute | solution.py:23
  19.8 20.0 %collective-permute-start.2 = (bf16[2,4,256,128]{3,2,1,0:T(8,128)(2,1)}, bf16[2,4,256,128]{3,2,1,0:T(8,128)(2,1)S(1)}, u32[]{:S(2)}, u32[]{:S(2)}) collective-permute-start(bf16[2,4,256,128]{3,2,1,0:T(8,128)(2,1)} %get-tuple-element.10), channel_id=1, source_target_pairs={{16,4},{24,12},{4,16},{32,20},{12,24},{40,28},{20,32},{48,36},{28,... | collective-permute-start | bytes 1572872 | tf_op jit(solution)/shard_map/ppermute | solution.py:23
  20.5 44.3 %collective-permute-start.3 = (bf16[2,4,256,128]{3,2,1,0:T(8,128)(2,1)}, bf16[2,4,256,128]{3,2,1,0:T(8,128)(2,1)}, u32[]{:S(2)}, u32[]{:S(2)}) collective-permute-start(bf16[2,4,256,128]{3,2,1,0:T(8,128)(2,1)} %get-tuple-element.10), channel_id=1, source_target_pairs={{20,4},{28,12},{0,16},{36,20},{8,24},{44,28},{16,32},{52,36},{24,4... | collective-permute-start | bytes 1572872 | tf_op jit(solution)/shard_map/ppermute | solution.py:23
  27.7 57.8 %collective-permute-start.10 = (bf16[512,2048]{1,0:T(8,128)(2,1)}, bf16[512,2048]{1,0:T(8,128)(2,1)}, u32[]{:S(2)}, u32[]{:S(2)}) collective-permute-start(bf16[512,2048]{1,0:T(8,128)(2,1)} %param.16), channel_id=1, source_target_pairs={{0,3},{1,0},{2,1},{3,2},{4,7},{5,4},{6,5},{7,6},{8,11},{9,8},{10,9... | collective-permute-start | bytes 6291464 | tf_op jit(solution)/shard_map/ppermute | solution.py:33
  28.7 97.9 %collective-permute-start.8 = (bf16[512,2048]{1,0:T(8,128)(2,1)}, bf16[512,2048]{1,0:T(8,128)(2,1)}, u32[]{:S(2)}, u32[]{:S(2)}) collective-permute-start(bf16[512,2048]{1,0:T(8,128)(2,1)} %param.16), channel_id=1, source_target_pairs={{0,1},{1,2},{2,3},{3,0},{4,5},{5,6},{6,7},{7,4},{8,9},{9,10},{10,1... | collective-permute-start | bytes 6291464 | tf_op jit(solution)/shard_map/ppermute | solution.py:33
  37.7 88.9 %collective-permute-start.9 = (bf16[512,2048]{1,0:T(8,128)(2,1)}, bf16[512,2048]{1,0:T(8,128)(2,1)}, u32[]{:S(2)}, u32[]{:S(2)}) collective-permute-start(bf16[512,2048]{1,0:T(8,128)(2,1)} %param.16), channel_id=1, source_target_pairs={{0,2},{1,3},{2,0},{3,1},{4,6},{5,7},{6,4},{7,5},{8,10},{9,11},{10,... | collective-permute-start | bytes 6291464 | tf_op jit(solution)/shard_map/ppermute | solution.py:33
  39.8 0.8 copy-start.2
  42.2 24.5 %collective-permute-start.4 = (bf16[4,2,4,256,128]{4,3,2,1,0:T(8,128)(2,1)}, bf16[4,2,4,256,128]{4,3,2,1,0:T(8,128)(2,1)S(1)}, u32[]{:S(2)}, u32[]{:S(2)}) collective-permute-start(bf16[4,2,4,256,128]{4,3,2,1,0:T(8,128)(2,1)} %pad_maximum_fusion), channel_id=1, source_target_pairs={{0,4},{4,0},{8,12},{12,8},{16,20},{20,16},{24,28},{28,24},{32,36},... | collective-permute-start | bytes 6291464 | tf_op jit(solution)/shard_map/ppermute | solution.py:118
  60.2 3.6 %copy-start.3 = (bf16[2,4,256,128]{3,2,1,0:T(8,128)(2,1)S(1)}, bf16[2,4,256,128]{3,2,1,0:T(8,128)(2,1)}, u32[]{:S(2)}) copy-start(bf16[2,4,256,128]{3,2,1,0:T(8,128)(2,1)} %copy-done.2) | copy-start | bytes 1572868
  66.7 3.6 %copy-start.7 = (pred[256,2304]{1,0:T(8,128)(4,1)S(1)}, pred[256,2304]{1,0:T(8,128)(4,1)}, u32[]{:S(2)}) copy-start(pred[256,2304]{1,0:T(8,128)(4,1)} %fusion.18) | copy-start | bytes 1769476
  75.2 56.1 %copy-start.5 = (bf16[256,2048]{1,0:T(8,128)(2,1)S(1)}, bf16[256,2048]{1,0:T(8,128)(2,1)}, u32[]{:S(2)}) copy-start(bf16[256,2048]{1,0:T(8,128)(2,1)} %param.12) | copy-start | bytes 3145732
  82.5 46.3 %collective-permute-start.5 = (bf16[256,512]{0,1:T(8,128)(2,1)S(1)}, bf16[256,512]{0,1:T(8,128)(2,1)S(1)}, u32[]{:S(2)}, u32[]{:S(2)}) collective-permute-start(bf16[256,512]{0,1:T(8,128)(2,1)S(1)} %bitcast.147), channel_id=1, source_target_pairs={{0,1},{1,2},{2,3},{3,0},{4,5},{5,6},{6,7},{7,4},{8,9},{9,10},{10,1... | collective-permute-start | bytes 786440 | tf_op jit(solution)/shard_map/ppermute | solution.py:33
  84.1 44.7 %collective-permute-start.6 = (bf16[256,512]{0,1:T(8,128)(2,1)S(1)}, bf16[256,512]{0,1:T(8,128)(2,1)S(1)}, u32[]{:S(2)}, u32[]{:S(2)}) collective-permute-start(bf16[256,512]{0,1:T(8,128)(2,1)S(1)} %bitcast.148), channel_id=1, source_target_pairs={{0,2},{1,3},{2,0},{3,1},{4,6},{5,7},{6,4},{7,5},{8,10},{9,11},{10,... | collective-permute-start | bytes 786440 | tf_op jit(solution)/shard_map/ppermute | solution.py:33
  85.4 45.8 %collective-permute-start.7 = (bf16[256,512]{0,1:T(8,128)(2,1)S(1)}, bf16[256,512]{0,1:T(8,128)(2,1)S(1)}, u32[]{:S(2)}, u32[]{:S(2)}) collective-permute-start(bf16[256,512]{0,1:T(8,128)(2,1)S(1)} %bitcast.149), channel_id=1, source_target_pairs={{0,3},{1,0},{2,1},{3,2},{4,7},{5,4},{6,5},{7,6},{8,11},{9,8},{10,9... | collective-permute-start | bytes 786440 | tf_op jit(solution)/shard_map/ppermute | solution.py:33
  126.7 9.6 %copy-start.8 = (f32[2048]{0:T(1024)S(1)}, f32[2048]{0:T(1024)}, u32[]{:S(2)}) copy-start(f32[2048]{0:T(1024)} %param.18) | copy-start | bytes 24580
  136.5 6.2 %copy-start.6 = (bf16[256,2048]{1,0:T(8,128)(2,1)}, bf16[256,2048]{1,0:T(8,128)(2,1)S(1)}, u32[]{:S(2)}) copy-start(bf16[256,2048]{1,0:T(8,128)(2,1)S(1)} %multiply_convert_fusion) | copy-start | bytes 3145732
  147.8 9.1 %copy-start.10 = (f32[1,128]{1,0:T(1,128)S(1)}, f32[1,128]{1,0:T(1,128)}, u32[]{:S(2)}) copy-start(f32[1,128]{1,0:T(1,128)} %param.22) | copy-start | bytes 1540
  147.8 2.1 collective-permute-start.11
  150.0 71.5 %copy-start.1 = (bf16[2048,512]{1,0:T(8,128)(2,1)S(1)}, bf16[2048,512]{1,0:T(8,128)(2,1)}, u32[]{:S(2)}) copy-start(bf16[2048,512]{1,0:T(8,128)(2,1)} %param.14) | copy-start | bytes 6291460
  153.0 9.8 %collective-permute-start.12 = (f32[16,32,128]{2,1,0:T(8,128)S(1)}, f32[16,32,128]{2,1,0:T(8,128)S(1)}, u32[]{:S(2)}, u32[]{:S(2)}) collective-permute-start(f32[16,32,128]{2,1,0:T(8,128)S(1)} %constant_dynamic-slice_fusion.3), channel_id=1, source_target_pairs={{0,8},{4,12},{8,0},{12,4},{16,24},{20,28},{24,16},{28,20},{32,40},... | collective-permute-start | bytes 786440 | tf_op jit(solution)/shard_map/ppermute | solution.py:28
  163.8 7.3 %collective-permute-start.13 = (f32[8,32,128]{2,1,0:T(8,128)S(1)}, f32[8,32,128]{2,1,0:T(8,128)S(1)}, u32[]{:S(2)}, u32[]{:S(2)}) collective-permute-start(f32[8,32,128]{2,1,0:T(8,128)S(1)} %constant_dynamic-slice_fusion.2), channel_id=1, source_target_pairs={{0,64},{4,68},{8,72},{12,76},{16,80},{20,84},{24,88},{28,92},{32,9... | collective-permute-start | bytes 393224 | tf_op jit(solution)/shard_map/ppermute | solution.py:28
  171.3 8.0 %collective-permute-start.14 = (f32[8,4225]{1,0:T(8,128)S(1)}, f32[8,4225]{1,0:T(8,128)S(1)}, u32[]{:S(2)}, u32[]{:S(2)}) collective-permute-start(f32[8,4225]{1,0:T(8,128)S(1)} %pad_maximum_fusion.2), channel_id=1, source_target_pairs={{0,16},{4,20},{8,24},{12,28},{16,0},{20,4},{24,8},{28,12},{32,48},... | collective-permute-start | bytes 405608 | tf_op jit(solution)/shard_map/ppermute | solution.py:28
  179.3 6.6 %collective-permute-start.15 = (f32[8,4225]{1,0:T(8,128)S(1)}, f32[8,4225]{1,0:T(8,128)S(1)}, u32[]{:S(2)}, u32[]{:S(2)}) collective-permute-start(f32[8,4225]{1,0:T(8,128)S(1)} %fusion.53), channel_id=1, source_target_pairs={{0,128},{4,132},{8,136},{12,140},{16,144},{20,148},{24,152},{28,15... | collective-permute-start | bytes 405608 | tf_op jit(solution)/shard_map/ppermute | solution.py:28
  186.0 9.2 %collective-permute-start.16 = (f32[8,4225]{1,0:T(8,128)S(1)}, f32[8,4225]{1,0:T(8,128)S(1)}, u32[]{:S(2)}, u32[]{:S(2)}) collective-permute-start(f32[8,4225]{1,0:T(8,128)S(1)} %max.64), channel_id=1, source_target_pairs={{0,32},{4,36},{8,40},{12,44},{16,48},{20,52},{24,56},{28,60},{32,0... | collective-permute-start | bytes 405608 | tf_op jit(solution)/shard_map/ppermute | solution.py:28
  196.9 1.3 collective-permute-start.17
  199.5 3.6 %collective-permute-start.18 = (f32[]{:T(128)}, f32[]{:T(128)}, u32[]{:S(2)}, u32[]{:S(2)}) collective-permute-start(f32[]{:T(128)} %add.191), channel_id=1, source_target_pairs={{0,8},{4,12},{8,0},{12,4},{16,24},{20,28},{24,16},{28,20},{32,40},... | collective-permute-start | bytes 20 | tf_op jit(solution)/shard_map/ppermute | solution.py:28
  203.8 3.6 %collective-permute-start.19 = (f32[]{:T(128)}, f32[]{:T(128)}, u32[]{:S(2)}, u32[]{:S(2)}) collective-permute-start(f32[]{:T(128)} %add.192), channel_id=1, source_target_pairs={{0,64},{4,68},{8,72},{12,76},{16,80},{20,84},{24,88},{28,92},{32,9... | collective-permute-start | bytes 20 | tf_op jit(solution)/shard_map/ppermute | solution.py:28
  208.1 6.8 %collective-permute-start.20 = (f32[]{:T(128)}, f32[]{:T(128)}, u32[]{:S(2)}, u32[]{:S(2)}) collective-permute-start(f32[]{:T(128)} %add.193), channel_id=1, source_target_pairs={{0,1},{1,0},{2,3},{3,2},{4,5},{5,4},{6,7},{7,6},{8,9},{9,8},{10,11... | collective-permute-start | bytes 20 | tf_op jit(solution)/shard_map/ppermute | solution.py:28
  215.6 5.1 %collective-permute-start.21 = (f32[]{:T(128)}, f32[]{:T(128)}, u32[]{:S(2)}, u32[]{:S(2)}) collective-permute-start(f32[]{:T(128)} %add.194), channel_id=1, source_target_pairs={{0,2},{1,3},{2,0},{3,1},{4,6},{5,7},{6,4},{7,5},{8,10},{9,11},{10,... | collective-permute-start | bytes 20 | tf_op jit(solution)/shard_map/ppermute | solution.py:28
Sparse Core Ops, SparseCore 0:
  10.8 98.5 all-gather.1

commit v2 on v1

--- a/solution.py
+++ b/solution.py
@@ -169,22 +169,23 @@
     own_count = queries.shape[0]
     group_bits = HALVING_BITS[3:]
     token_max = halving_max(part_max, "seq", len(HALVING_BITS) - len(group_bits))
+    for bit in group_bits:
+        token_max = jnp.maximum(token_max, xor_swap(token_max, "seq", bit))
+    side_row = jnp.concatenate([teacher, query_lengths.astype(jnp.float32)[:, None]], axis=1)
     member = 0
     for bit in group_bits:
         member = member * 2 + ((seq_place & bit) != 0).astype(jnp.int32)
-    group_size = 2 ** len(group_bits)
-    side_row = jnp.concatenate([teacher, query_lengths.astype(jnp.float32)[:, None]], axis=1)
-    side_rows = jnp.where(
-        (jnp.arange(group_size, dtype=jnp.int32) == member)[:, None],
-        jnp.broadcast_to(side_row, (group_size, side_row.shape[1])),
-        -jnp.inf,
-    )
-    slot_width = token_max.shape[1] * token_max.shape[2]
-    packed = jnp.concatenate([token_max.reshape(group_size, slot_width), side_rows], axis=1)
-    for bit in group_bits:
-        packed = jnp.maximum(packed, xor_swap(packed, "seq", bit))
-    token_max = packed[:, :slot_width].reshape(group_size, *part_max.shape[1:])
-    side_rows = packed[:, slot_width:]
+    side_parts = [side_row]
+    for offset in range(1, 2 ** len(group_bits)):
+        mask = 0
+        for place, bit in enumerate(group_bits[::-1]):
+            if (offset >> place) & 1:
+                mask |= bit
+        side_parts.append(xor_swap(side_row, "seq", mask))
+    side_stack = jnp.concatenate(side_parts, axis=0)
+    side_rows = jnp.take(
+        side_stack, member ^ jnp.arange(2 ** len(group_bits), dtype=jnp.int32), axis=0
+    )
     group_teacher = side_rows[:, :-1]
     group_lengths_f = side_rows[:, -1]
     live_mask = (
@@ -202,7 +203,7 @@
     teacher_prob = jnp.exp(log_t)
     kl_terms = jnp.sum(teacher_prob * (log_t - student_log_prob), axis=-1)
     query_count_all = own_count * seq_count * lax.axis_size("pb")
-    loss_sum = butterfly_sum(butterfly_sum(jnp.sum(kl_terms), "seq", HALVING_BITS[:3]), "pb")
+    loss_sum = lax.psum(butterfly_sum(jnp.sum(kl_terms), "seq", HALVING_BITS[:3]), "pb")
     distill_loss = loss_sum / query_count_all
     gradient_rows = (jnp.exp(student_log_prob) - teacher_prob) / (SOFTMAX_TEMP * query_count_all)
     scores = lax.dynamic_slice_in_dim(group_scores, member, 1, 0)

time: 232 us -> 247 us (1.065)
  blocking collectives: 0 us -> 13.3 us
  starting transfers between devices: 108 us -> 112 us
    psum x0 -> x1, blocking collectives: none -> 13.3 us  [per_device(): lax.psum(butterfly_sum(jnp.sum(kl_terms), 'seq', HALVING_BITS[:3]), 'pb')]
    ppermute x11 -> x16, starting transfers between devices: 30.5 us -> 34.4 us  [xor_swap(): return lax.ppermute(x, axis, [(i, i ^ bit) for i in range(count)])]
    ppermute x11 -> x16, waiting for transfers between devices: 31.2 us -> 30.5 us  [xor_swap(): return lax.ppermute(x, axis, [(i, i ^ bit) for i in range(count)])]
    unnamed x36 -> x35, local copies, waits for them, and re-layouts: 8.35 us -> 8.27 us
  transfers between devices with their start and end apart: 23 -> 28, of which waited for: 14 -> 12; matrix products, arithmetic and copies ran while one was open for 17% -> 17% of each run, Pallas kernels for 0% -> 0%
where the time goes in v2:
time: 247 us; the launch traced here: 246 us
  starting transfers between devices  112 us (45%)
  waiting for transfers between devices  43.3 us (18%)
  matrix products  28.8 us (12%)
  between operations  19.7 us (8%)
  local copies, waits for them, and re-layouts  15.2 us (6%)
  other arithmetic  14.6 us (6%)
  blocking collectives  13.3 us (5%)
    ppermute x6, starting transfers between devices, ring_shift(): return lax.ppermute(x, axis, [(i, (i + by) % count) for i in range(count)])  48.2 us
    ppermute x16, starting transfers between devices, xor_swap(): return lax.ppermute(x, axis, [(i, i ^ bit) for i in range(count)])  34.4 us
    ppermute x16, waiting for transfers between devices, xor_swap(): return lax.ppermute(x, axis, [(i, i ^ bit) for i in range(count)])  30.5 us
    ppermute x1, starting transfers between devices, per_device(): lax.ppermute(jnp.stack([key_value] + fetched[:reach_count - 1]), 'seq', [...  15.3 us
    ppermute x4, starting transfers between devices, sided_fetch(): return lax.ppermute(x, axis, pairs)  13.6 us
    psum x1, blocking collectives, per_device(): lax.psum(butterfly_sum(jnp.sum(kl_terms), 'seq', HALVING_BITS[:3]), 'pb')  13.3 us
    unnamed x35, local copies, waits for them, and re-layouts  8.27 us
    ppermute x4, waiting for transfers between devices, sided_fetch(): return lax.ppermute(x, axis, pairs)  7.5 us
  transfers between devices with their start and end apart: 28, of which 12 were waited for; matrix products, arithmetic and copies ran while one was open for 17% of the time, Pallas kernels for 0%

profile of v2, /device:TPU:2, one launch (start us, length us, event | category | flops | bytes accessed | tf_op | source)
XLA Modules:
  0.0 246.4 jit_solution(6302726050527247658)
XLA Ops:
  7.2 0.7 all-gather.2.cloned.1.call-update
  7.9 1.5 fusion.19
  9.5 2.1 fusion.23
  11.7 0.8 fusion.24
  12.6 1.4 fusion.52
  14.0 0.7 collective-permute-start
  14.7 5.1 %collective-permute-start.1 = (bf16[2,4,256,128]{3,2,1,0:T(8,128)(2,1)}, bf16[2,4,256,128]{3,2,1,0:T(8,128)(2,1)S(1)}, u32[]{:S(2)}, u32[]{:S(2)}) collective-permute-start(bf16[2,4,256,128]{3,2,1,0:T(8,128)(2,1)} %get-tuple-element.10), channel_id=1, source_target_pairs={{12,4},{0,8},{20,12},{8,16},{28,20},{16,24},{36,28},{24,32},{44,36... | collective-permute-start | bytes 1572872 | tf_op jit(solution)/shard_map/ppermute | solution.py:23
  19.8 0.7 collective-permute-start.2
  20.5 7.2 %collective-permute-start.3 = (bf16[2,4,256,128]{3,2,1,0:T(8,128)(2,1)}, bf16[2,4,256,128]{3,2,1,0:T(8,128)(2,1)}, u32[]{:S(2)}, u32[]{:S(2)}) collective-permute-start(bf16[2,4,256,128]{3,2,1,0:T(8,128)(2,1)} %get-tuple-element.10), channel_id=1, source_target_pairs={{20,4},{28,12},{0,16},{36,20},{8,24},{44,28},{16,32},{52,36},{24,4... | collective-permute-start | bytes 1572872 | tf_op jit(solution)/shard_map/ppermute | solution.py:23
  28.7 1.5 collective-permute-start.8
  30.2 7.5 %collective-permute-done.1 = bf16[2,4,256,128]{3,2,1,0:T(8,128)(2,1)S(1)} collective-permute-done((bf16[2,4,256,128]{3,2,1,0:T(8,128)(2,1)}, bf16[2,4,256,128]{3,2,1,0:T(8,128)(2,1)S(1)}, u32[]{:S(2)}, u32[]{:S(2)}) %collective-permute-start.1) | collective-permute-done | bytes 524320 | tf_op jit(solution)/shard_map/ppermute | solution.py:23
  37.7 2.1 collective-permute-start.9
  39.8 0.8 copy-done.2
  40.7 1.6 pad_maximum_fusion
  42.2 15.3 %collective-permute-start.4 = (bf16[4,2,4,256,128]{4,3,2,1,0:T(8,128)(2,1)}, bf16[4,2,4,256,128]{4,3,2,1,0:T(8,128)(2,1)S(1)}, u32[]{:S(2)}, u32[]{:S(2)}) collective-permute-start(bf16[4,2,4,256,128]{4,3,2,1,0:T(8,128)(2,1)} %pad_maximum_fusion), channel_id=1, source_target_pairs={{0,4},{4,0},{8,12},{12,8},{16,20},{20,16},{24,28},{28,24},{32,36},... | collective-permute-start | bytes 6291464 | tf_op jit(solution)/shard_map/ppermute | solution.py:118
  57.5 2.7 %fusion.25 = bf16[32,4,8,128]{3,2,1,0:T(8,128)(2,1)S(1)} fusion(bf16[2048,512]{1,0:T(8,128)(2,1)} %param.13, bf16[256,2048]{1,0:T(8,128)(2,1)} %param.12, f32[2048]{0:T(1024)S(1)} %copy-done.13, f32[256]{0:T(256)S(1)} %add_rsqrt_fusion.1), kind=kOutput, calls=%fused_computation.49 | convolution fusion | flops 539099136 | bytes 3417088 | tf_op jit(solution)/shard_map/dot_general | solution.py:109
  60.2 1.7 fusion.18
  62.1 0.9 constant_dynamic-update-slice_fusion.3
  63.0 0.9 constant_dynamic-update-slice_fusion.2
  63.9 0.9 constant_dynamic-update-slice_fusion.1
  64.8 1.9 constant_dynamic-update-slice_fusion
  66.7 0.9 fusion.36
  67.6 0.9 fusion.35
  68.5 0.9 fusion.34
  69.4 0.9 fusion.33
  70.3 4.9 %fusion.56 = f32[4,256]{1,0:T(4,128)S(1)} fusion(pred[256,2304]{1,0:T(8,128)(4,1)S(1)} %copy-done.7, bf16[2,4,2304,128]{3,2,1,0:T(8,128)(2,1)} %fusion.33, bf16[32,4,8,128]{3,2,1,0:T(8,128)(2,1)S(1)} %fusion.25), kind=kOutput, calls=%fused_computation.135 | convolution fusion | flops 613419264 | bytes 3215360 | tf_op jit(solution)/shard_map/sub | solution.py:145
  75.2 7.3 %fusion.22 = bf16[4,128,256]{2,1,0:T(8,128)(2,1)S(1)} fusion(f32[4,256]{1,0:T(4,128)S(1)} %fusion.56, bf16[2,4,2304,128]{3,2,1,0:T(8,128)(2,1)} %fusion.33, pred[256,2304]{1,0:T(8,128)(4,1)S(1)} %copy-done.7, bf16[32,4,8,128]{3,2,1,0:T(8,128)(2,1)S(1)} %fusion.25), kind=kOutput, calls=%fused_computation.43 | convolution fusion | flops 1219890432 | bytes 5836800 | tf_op jit(solution)/shard_map/hqk,hkd->qhd/dot_general | solution.py:147
  82.5 1.7 collective-permute-start.5
  84.1 1.3 collective-permute-start.6
  85.4 41.1 %collective-permute-start.7 = (bf16[256,512]{0,1:T(8,128)(2,1)S(1)}, bf16[256,512]{0,1:T(8,128)(2,1)S(1)}, u32[]{:S(2)}, u32[]{:S(2)}) collective-permute-start(bf16[256,512]{0,1:T(8,128)(2,1)S(1)} %bitcast.136), channel_id=1, source_target_pairs={{0,3},{1,0},{2,1},{3,2},{4,7},{5,4},{6,5},{7,6},{8,11},{9,8},{10,9... | collective-permute-start | bytes 786440 | tf_op jit(solution)/shard_map/ppermute | solution.py:33
  126.7 2.1 collective-permute-done.5
  128.8 2.5 %collective-permute-done.7 = bf16[256,512]{0,1:T(8,128)(2,1)S(1)} collective-permute-done((bf16[256,512]{0,1:T(8,128)(2,1)S(1)}, bf16[256,512]{0,1:T(8,128)(2,1)S(1)}, u32[]{:S(2)}, u32[]{:S(2)}) %collective-permute-start.7) | collective-permute-done | bytes 262176 | tf_op jit(solution)/shard_map/ppermute | solution.py:33
  131.3 4.9 %multiply_reduce_fusion = (f32[256]{0:T(256)S(1)}, f32[256,2048]{1,0:T(8,128)S(1)}) fusion(bf16[512,2048]{1,0:T(8,128)(2,1)} %collective-permute-done.10, bf16[512,2048]{1,0:T(8,128)(2,1)} %collective-permute-done.9, bf16[512,2048]{1,0:T(8,128)(2,1)} %collective-permute-done.8, bf16[512,2048]{1,0:T(8,128)(2,1)} %param.16, ...), kind=kOutput, calls=%fused_computation.42 | convolution fusion | flops 2187329280 | bytes 12583936 | tf_op jit(solution)/shard_map/dot_general | solution.py:150
  136.5 6.1 %convolution_bitcast_fusion = f32[2048,256]{0,1:T(8,128)S(1)} fusion(bf16[256,2048]{1,0:T(8,128)(2,1)S(1)} %multiply_convert_fusion, bf16[2048,2048]{1,0:T(8,128)(2,1)} %bitcast.133), kind=kOutput, calls=%fused_computation.30 | convolution fusion | flops 2147483648 | bytes 11534336 | tf_op jit(solution)/shard_map/td,rd->tr/dot_general | solution.py:164
  146.2 1.0 gather_fusion
  147.8 0.9 constant_dynamic-slice_fusion.4
  148.6 2.2 collective-permute-done.11
  150.9 1.9 dynamic-slice_maximum_fusion
  152.8 1.0 constant_dynamic-slice_fusion.3
  153.8 3.2 %collective-permute-start.12 = (f32[16,32,128]{2,1,0:T(8,128)S(1)}, f32[16,32,128]{2,1,0:T(8,128)S(1)}, u32[]{:S(2)}, u32[]{:S(2)}) collective-permute-start(f32[16,32,128]{2,1,0:T(8,128)S(1)} %constant_dynamic-slice_fusion.3), channel_id=1, source_target_pairs={{0,8},{4,12},{8,0},{12,4},{16,24},{20,28},{24,16},{28,20},{32,40},... | collective-permute-start | bytes 786440 | tf_op jit(solution)/shard_map/ppermute | solution.py:28
  157.7 5.9 %collective-permute-start.17 = (f32[1,129]{1,0:T(1,128)S(1)}, f32[1,129]{1,0:T(1,128)S(1)}, u32[]{:S(2)}, u32[]{:S(2)}) collective-permute-start(f32[1,129]{1,0:T(1,128)S(1)} %pad_maximum_fusion.2), channel_id=1, source_target_pairs={{0,32},{4,36},{8,40},{12,44},{16,48},{20,52},{24,56},{28,60},{32,0... | collective-permute-start | bytes 1556 | tf_op jit(solution)/shard_map/ppermute | solution.py:28
  163.6 3.2 %collective-permute-start.18 = (f32[1,129]{1,0:T(1,128)S(1)}, f32[1,129]{1,0:T(1,128)S(1)}, u32[]{:S(2)}, u32[]{:S(2)}) collective-permute-start(f32[1,129]{1,0:T(1,128)S(1)} %pad_maximum_fusion.2), channel_id=1, source_target_pairs={{0,128},{4,132},{8,136},{12,140},{16,144},{20,148},{24,152},{28,15... | collective-permute-start | bytes 1556 | tf_op jit(solution)/shard_map/ppermute | solution.py:28
  167.3 2.6 %collective-permute-start.20 = (f32[1,129]{1,0:T(1,128)S(1)}, f32[1,129]{1,0:T(1,128)S(1)}, u32[]{:S(2)}, u32[]{:S(2)}) collective-permute-start(f32[1,129]{1,0:T(1,128)S(1)} %pad_maximum_fusion.2), channel_id=1, source_target_pairs={{0,16},{4,20},{8,24},{12,28},{16,0},{20,4},{24,8},{28,12},{32,48},... | collective-permute-start | bytes 1556 | tf_op jit(solution)/shard_map/ppermute | solution.py:28
  169.9 1.0 dynamic-slice_maximum_fusion.1
  170.9 1.7 collective-permute-start.13
  172.6 3.5 %collective-permute-start.21 = (f32[1,129]{1,0:T(1,128)S(1)}, f32[1,129]{1,0:T(1,128)S(1)}, u32[]{:S(2)}, u32[]{:S(2)}) collective-permute-start(f32[1,129]{1,0:T(1,128)S(1)} %pad_maximum_fusion.2), channel_id=1, source_target_pairs={{0,48},{4,52},{8,56},{12,60},{16,32},{20,36},{24,40},{28,44},{32,1... | collective-permute-start | bytes 1556 | tf_op jit(solution)/shard_map/ppermute | solution.py:28
  176.1 3.5 %collective-permute-start.22 = (f32[1,129]{1,0:T(1,128)S(1)}, f32[1,129]{1,0:T(1,128)S(1)}, u32[]{:S(2)}, u32[]{:S(2)}) collective-permute-start(f32[1,129]{1,0:T(1,128)S(1)} %pad_maximum_fusion.2), channel_id=1, source_target_pairs={{0,144},{4,148},{8,152},{12,156},{16,128},{20,132},{24,136},{28,14... | collective-permute-start | bytes 1556 | tf_op jit(solution)/shard_map/ppermute | solution.py:28
  179.6 1.4 collective-permute-start.23
  181.0 2.0 collective-permute-done.22
  183.0 4.7 %collective-permute-done.23 = f32[1,129]{1,0:T(1,128)S(1)} collective-permute-done((f32[1,129]{1,0:T(1,128)S(1)}, f32[1,129]{1,0:T(1,128)S(1)}, u32[]{:S(2)}, u32[]{:S(2)}) %collective-permute-start.23) | collective-permute-done | bytes 548 | tf_op jit(solution)/shard_map/ppermute | solution.py:28
  187.7 0.6 gather_fusion.1
  188.3 2.1 collective-permute-start.14
  190.5 5.1 %collective-permute-done.14 = f32[8,32,128]{2,1,0:T(8,128)S(1)} collective-permute-done((f32[8,32,128]{2,1,0:T(8,128)S(1)}, f32[8,32,128]{2,1,0:T(8,128)S(1)}, u32[]{:S(2)}, u32[]{:S(2)}) %collective-permute-start.14) | collective-permute-done | bytes 131104 | tf_op jit(solution)/shard_map/ppermute | solution.py:28
  195.7 1.4 collective-permute-start.15
  197.3 5.0 %collective-permute-done.15 = f32[8,32,128]{2,1,0:T(8,128)S(1)} collective-permute-done((f32[8,32,128]{2,1,0:T(8,128)S(1)}, f32[8,32,128]{2,1,0:T(8,128)S(1)}, u32[]{:S(2)}, u32[]{:S(2)}) %collective-permute-start.15) | collective-permute-done | bytes 131104 | tf_op jit(solution)/shard_map/ppermute | solution.py:28
  202.2 2.1 collective-permute-start.16
  204.6 7.0 %collective-permute-done.16 = f32[8,32,128]{2,1,0:T(8,128)S(1)} collective-permute-done((f32[8,32,128]{2,1,0:T(8,128)S(1)}, f32[8,32,128]{2,1,0:T(8,128)S(1)}, u32[]{:S(2)}, u32[]{:S(2)}) %collective-permute-start.16) | collective-permute-done | bytes 131104 | tf_op jit(solution)/shard_map/ppermute | solution.py:28
  212.1 0.7 multiply_reduce_fusion.2
  213.3 0.8 collective-permute-done.24
  215.4 1.4 collective-permute-start.25
  216.8 2.2 collective-permute-done.25
  219.7 2.0 collective-permute-start.26
  221.7 1.6 collective-permute-done.26
  224.5 13.3 %psum.7 = f32[]{:T(128)} all-reduce(f32[]{:T(128)S(6)} %add.206), channel_id=1, replica_groups=mesh['seq'=64,'pb'=4] {'pb'}, use_global_device_ids=true, to_apply=%region_12.13 | all-reduce | flops 1 | bytes 8 | tf_op jit(solution)/shard_map/psum | solution.py:206
  (103 shorter events, 8.8 us)
Async XLA Ops:
  7.2 2.3 copy-start
  7.2 129.4 %all-gather.2.cloned.1.call-start = ((), (), s32[]{:S(2)}) async-start(), calls=%async_computation | async-start | bytes 8519680 | tf_op jit(solution)/shard_map/all_gather | solution.py:161
  9.4 2.2 copy-start.4
  9.5 2.2 copy-start.12
  9.5 2.2 copy-start.13
  12.5 15.8 %copy-start.9 = (s32[128]{0:T(128)S(1)}, s32[128]{0:T(128)}, u32[]{:S(2)}) copy-start(s32[128]{0:T(128)} %param.21) | copy-start | bytes 1540
  12.5 16.1 %copy-start.11 = (s32[9]{0:T(128)S(1)}, s32[9]{0:T(128)}, u32[]{:S(2)}) copy-start(s32[9]{0:T(128)} %constant.124.clone) | copy-start | bytes 112
  14.0 14.7 %collective-permute-start = (bf16[2,4,256,128]{3,2,1,0:T(8,128)(2,1)}, bf16[2,4,256,128]{3,2,1,0:T(8,128)(2,1)S(1)}, u32[]{:S(2)}, u32[]{:S(2)}) collective-permute-start(bf16[2,4,256,128]{3,2,1,0:T(8,128)(2,1)} %get-tuple-element.10), channel_id=1, source_target_pairs={{8,4},{4,8},{16,12},{12,16},{24,20},{20,24},{32,28},{28,32},{40,36... | collective-permute-start | bytes 1572872 | tf_op jit(solution)/shard_map/ppermute | solution.py:23
  14.7 23.0 %collective-permute-start.1 = (bf16[2,4,256,128]{3,2,1,0:T(8,128)(2,1)}, bf16[2,4,256,128]{3,2,1,0:T(8,128)(2,1)S(1)}, u32[]{:S(2)}, u32[]{:S(2)}) collective-permute-start(bf16[2,4,256,128]{3,2,1,0:T(8,128)(2,1)} %get-tuple-element.10), channel_id=1, source_target_pairs={{12,4},{0,8},{20,12},{8,16},{28,20},{16,24},{36,28},{24,32},{44,36... | collective-permute-start | bytes 1572872 | tf_op jit(solution)/shard_map/ppermute | solution.py:23
  19.8 20.0 %collective-permute-start.2 = (bf16[2,4,256,128]{3,2,1,0:T(8,128)(2,1)}, bf16[2,4,256,128]{3,2,1,0:T(8,128)(2,1)S(1)}, u32[]{:S(2)}, u32[]{:S(2)}) collective-permute-start(bf16[2,4,256,128]{3,2,1,0:T(8,128)(2,1)} %get-tuple-element.10), channel_id=1, source_target_pairs={{16,4},{24,12},{4,16},{32,20},{12,24},{40,28},{20,32},{48,36},{28,... | collective-permute-start | bytes 1572872 | tf_op jit(solution)/shard_map/ppermute | solution.py:23
  20.5 44.3 %collective-permute-start.3 = (bf16[2,4,256,128]{3,2,1,0:T(8,128)(2,1)}, bf16[2,4,256,128]{3,2,1,0:T(8,128)(2,1)}, u32[]{:S(2)}, u32[]{:S(2)}) collective-permute-start(bf16[2,4,256,128]{3,2,1,0:T(8,128)(2,1)} %get-tuple-element.10), channel_id=1, source_target_pairs={{20,4},{28,12},{0,16},{36,20},{8,24},{44,28},{16,32},{52,36},{24,4... | collective-permute-start | bytes 1572872 | tf_op jit(solution)/shard_map/ppermute | solution.py:23
  27.7 57.8 %collective-permute-start.10 = (bf16[512,2048]{1,0:T(8,128)(2,1)}, bf16[512,2048]{1,0:T(8,128)(2,1)}, u32[]{:S(2)}, u32[]{:S(2)}) collective-permute-start(bf16[512,2048]{1,0:T(8,128)(2,1)} %param.16), channel_id=1, source_target_pairs={{0,3},{1,0},{2,1},{3,2},{4,7},{5,4},{6,5},{7,6},{8,11},{9,8},{10,9... | collective-permute-start | bytes 6291464 | tf_op jit(solution)/shard_map/ppermute | solution.py:33
  28.7 97.9 %collective-permute-start.8 = (bf16[512,2048]{1,0:T(8,128)(2,1)}, bf16[512,2048]{1,0:T(8,128)(2,1)}, u32[]{:S(2)}, u32[]{:S(2)}) collective-permute-start(bf16[512,2048]{1,0:T(8,128)(2,1)} %param.16), channel_id=1, source_target_pairs={{0,1},{1,2},{2,3},{3,0},{4,5},{5,6},{6,7},{7,4},{8,9},{9,10},{10,1... | collective-permute-start | bytes 6291464 | tf_op jit(solution)/shard_map/ppermute | solution.py:33
  37.7 88.9 %collective-permute-start.9 = (bf16[512,2048]{1,0:T(8,128)(2,1)}, bf16[512,2048]{1,0:T(8,128)(2,1)}, u32[]{:S(2)}, u32[]{:S(2)}) collective-permute-start(bf16[512,2048]{1,0:T(8,128)(2,1)} %param.16), channel_id=1, source_target_pairs={{0,2},{1,3},{2,0},{3,1},{4,6},{5,7},{6,4},{7,5},{8,10},{9,11},{10,... | collective-permute-start | bytes 6291464 | tf_op jit(solution)/shard_map/ppermute | solution.py:33
  39.8 0.8 copy-start.2
  42.2 24.5 %collective-permute-start.4 = (bf16[4,2,4,256,128]{4,3,2,1,0:T(8,128)(2,1)}, bf16[4,2,4,256,128]{4,3,2,1,0:T(8,128)(2,1)S(1)}, u32[]{:S(2)}, u32[]{:S(2)}) collective-permute-start(bf16[4,2,4,256,128]{4,3,2,1,0:T(8,128)(2,1)} %pad_maximum_fusion), channel_id=1, source_target_pairs={{0,4},{4,0},{8,12},{12,8},{16,20},{20,16},{24,28},{28,24},{32,36},... | collective-permute-start | bytes 6291464 | tf_op jit(solution)/shard_map/ppermute | solution.py:118
  60.2 3.6 %copy-start.3 = (bf16[2,4,256,128]{3,2,1,0:T(8,128)(2,1)S(1)}, bf16[2,4,256,128]{3,2,1,0:T(8,128)(2,1)}, u32[]{:S(2)}) copy-start(bf16[2,4,256,128]{3,2,1,0:T(8,128)(2,1)} %copy-done.2) | copy-start | bytes 1572868
  66.7 3.6 %copy-start.7 = (pred[256,2304]{1,0:T(8,128)(4,1)S(1)}, pred[256,2304]{1,0:T(8,128)(4,1)}, u32[]{:S(2)}) copy-start(pred[256,2304]{1,0:T(8,128)(4,1)} %fusion.18) | copy-start | bytes 1769476
  75.2 56.1 %copy-start.5 = (bf16[256,2048]{1,0:T(8,128)(2,1)S(1)}, bf16[256,2048]{1,0:T(8,128)(2,1)}, u32[]{:S(2)}) copy-start(bf16[256,2048]{1,0:T(8,128)(2,1)} %param.12) | copy-start | bytes 3145732
  82.5 46.3 %collective-permute-start.5 = (bf16[256,512]{0,1:T(8,128)(2,1)S(1)}, bf16[256,512]{0,1:T(8,128)(2,1)S(1)}, u32[]{:S(2)}, u32[]{:S(2)}) collective-permute-start(bf16[256,512]{0,1:T(8,128)(2,1)S(1)} %bitcast.134), channel_id=1, source_target_pairs={{0,1},{1,2},{2,3},{3,0},{4,5},{5,6},{6,7},{7,4},{8,9},{9,10},{10,1... | collective-permute-start | bytes 786440 | tf_op jit(solution)/shard_map/ppermute | solution.py:33
  84.1 44.7 %collective-permute-start.6 = (bf16[256,512]{0,1:T(8,128)(2,1)S(1)}, bf16[256,512]{0,1:T(8,128)(2,1)S(1)}, u32[]{:S(2)}, u32[]{:S(2)}) collective-permute-start(bf16[256,512]{0,1:T(8,128)(2,1)S(1)} %bitcast.135), channel_id=1, source_target_pairs={{0,2},{1,3},{2,0},{3,1},{4,6},{5,7},{6,4},{7,5},{8,10},{9,11},{10,... | collective-permute-start | bytes 786440 | tf_op jit(solution)/shard_map/ppermute | solution.py:33
  85.4 45.8 %collective-permute-start.7 = (bf16[256,512]{0,1:T(8,128)(2,1)S(1)}, bf16[256,512]{0,1:T(8,128)(2,1)S(1)}, u32[]{:S(2)}, u32[]{:S(2)}) collective-permute-start(bf16[256,512]{0,1:T(8,128)(2,1)S(1)} %bitcast.136), channel_id=1, source_target_pairs={{0,3},{1,0},{2,1},{3,2},{4,7},{5,4},{6,5},{7,6},{8,11},{9,8},{10,9... | collective-permute-start | bytes 786440 | tf_op jit(solution)/shard_map/ppermute | solution.py:33
  126.7 9.6 %copy-start.8 = (f32[2048]{0:T(1024)S(1)}, f32[2048]{0:T(1024)}, u32[]{:S(2)}) copy-start(f32[2048]{0:T(1024)} %param.18) | copy-start | bytes 24580
  136.5 6.2 %copy-start.6 = (bf16[256,2048]{1,0:T(8,128)(2,1)}, bf16[256,2048]{1,0:T(8,128)(2,1)S(1)}, u32[]{:S(2)}) copy-start(bf16[256,2048]{1,0:T(8,128)(2,1)S(1)} %multiply_convert_fusion) | copy-start | bytes 3145732
  147.8 9.9 %copy-start.10 = (f32[1,128]{1,0:T(1,128)S(1)}, f32[1,128]{1,0:T(1,128)}, u32[]{:S(2)}) copy-start(f32[1,128]{1,0:T(1,128)} %param.22) | copy-start | bytes 1540
  148.6 2.3 collective-permute-start.11
  148.6 89.8 %copy-start.1 = (bf16[2048,512]{1,0:T(8,128)(2,1)S(1)}, bf16[2048,512]{1,0:T(8,128)(2,1)}, u32[]{:S(2)}) copy-start(bf16[2048,512]{1,0:T(8,128)(2,1)} %param.14) | copy-start | bytes 6291460
  153.8 16.1 %collective-permute-start.12 = (f32[16,32,128]{2,1,0:T(8,128)S(1)}, f32[16,32,128]{2,1,0:T(8,128)S(1)}, u32[]{:S(2)}, u32[]{:S(2)}) collective-permute-start(f32[16,32,128]{2,1,0:T(8,128)S(1)} %constant_dynamic-slice_fusion.3), channel_id=1, source_target_pairs={{0,8},{4,12},{8,0},{12,4},{16,24},{20,28},{24,16},{28,20},{32,40},... | collective-permute-start | bytes 786440 | tf_op jit(solution)/shard_map/ppermute | solution.py:28
  157.7 14.9 %collective-permute-start.17 = (f32[1,129]{1,0:T(1,128)S(1)}, f32[1,129]{1,0:T(1,128)S(1)}, u32[]{:S(2)}, u32[]{:S(2)}) collective-permute-start(f32[1,129]{1,0:T(1,128)S(1)} %pad_maximum_fusion.2), channel_id=1, source_target_pairs={{0,32},{4,36},{8,40},{12,44},{16,48},{20,52},{24,56},{28,60},{32,0... | collective-permute-start | bytes 1556 | tf_op jit(solution)/shard_map/ppermute | solution.py:28
  163.6 12.5 %collective-permute-start.18 = (f32[1,129]{1,0:T(1,128)S(1)}, f32[1,129]{1,0:T(1,128)S(1)}, u32[]{:S(2)}, u32[]{:S(2)}) collective-permute-start(f32[1,129]{1,0:T(1,128)S(1)} %pad_maximum_fusion.2), channel_id=1, source_target_pairs={{0,128},{4,132},{8,136},{12,140},{16,144},{20,148},{24,152},{28,15... | collective-permute-start | bytes 1556 | tf_op jit(solution)/shard_map/ppermute | solution.py:28
  166.8 12.8 %collective-permute-start.19 = (f32[1,129]{1,0:T(1,128)S(1)}, f32[1,129]{1,0:T(1,128)S(1)}, u32[]{:S(2)}, u32[]{:S(2)}) collective-permute-start(f32[1,129]{1,0:T(1,128)S(1)} %pad_maximum_fusion.2), channel_id=1, source_target_pairs={{0,160},{4,164},{8,168},{12,172},{16,176},{20,180},{24,184},{28,18... | collective-permute-start | bytes 1556 | tf_op jit(solution)/shard_map/ppermute | solution.py:28
  167.3 13.7 %collective-permute-start.20 = (f32[1,129]{1,0:T(1,128)S(1)}, f32[1,129]{1,0:T(1,128)S(1)}, u32[]{:S(2)}, u32[]{:S(2)}) collective-permute-start(f32[1,129]{1,0:T(1,128)S(1)} %pad_maximum_fusion.2), channel_id=1, source_target_pairs={{0,16},{4,20},{8,24},{12,28},{16,0},{20,4},{24,8},{28,12},{32,48},... | collective-permute-start | bytes 1556 | tf_op jit(solution)/shard_map/ppermute | solution.py:28
  170.9 17.3 %collective-permute-start.13 = (f32[8,32,128]{2,1,0:T(8,128)S(1)}, f32[8,32,128]{2,1,0:T(8,128)S(1)}, u32[]{:S(2)}, u32[]{:S(2)}) collective-permute-start(f32[8,32,128]{2,1,0:T(8,128)S(1)} %constant_dynamic-slice_fusion.2), channel_id=1, source_target_pairs={{0,64},{4,68},{8,72},{12,76},{16,80},{20,84},{24,88},{28,92},{32,9... | collective-permute-start | bytes 393224 | tf_op jit(solution)/shard_map/ppermute | solution.py:28
  172.6 8.4 %collective-permute-start.21 = (f32[1,129]{1,0:T(1,128)S(1)}, f32[1,129]{1,0:T(1,128)S(1)}, u32[]{:S(2)}, u32[]{:S(2)}) collective-permute-start(f32[1,129]{1,0:T(1,128)S(1)} %pad_maximum_fusion.2), channel_id=1, source_target_pairs={{0,48},{4,52},{8,56},{12,60},{16,32},{20,36},{24,40},{28,44},{32,1... | collective-permute-start | bytes 1556 | tf_op jit(solution)/shard_map/ppermute | solution.py:28
  176.1 6.9 %collective-permute-start.22 = (f32[1,129]{1,0:T(1,128)S(1)}, f32[1,129]{1,0:T(1,128)S(1)}, u32[]{:S(2)}, u32[]{:S(2)}) collective-permute-start(f32[1,129]{1,0:T(1,128)S(1)} %pad_maximum_fusion.2), channel_id=1, source_target_pairs={{0,144},{4,148},{8,152},{12,156},{16,128},{20,132},{24,136},{28,14... | collective-permute-start | bytes 1556 | tf_op jit(solution)/shard_map/ppermute | solution.py:28
  179.6 8.1 %collective-permute-start.23 = (f32[1,129]{1,0:T(1,128)S(1)}, f32[1,129]{1,0:T(1,128)S(1)}, u32[]{:S(2)}, u32[]{:S(2)}) collective-permute-start(f32[1,129]{1,0:T(1,128)S(1)} %pad_maximum_fusion.2), channel_id=1, source_target_pairs={{0,176},{4,180},{8,184},{12,188},{16,160},{20,164},{24,168},{28,17... | collective-permute-start | bytes 1556 | tf_op jit(solution)/shard_map/ppermute | solution.py:28
  188.3 7.4 %collective-permute-start.14 = (f32[8,32,128]{2,1,0:T(8,128)S(1)}, f32[8,32,128]{2,1,0:T(8,128)S(1)}, u32[]{:S(2)}, u32[]{:S(2)}) collective-permute-start(f32[8,32,128]{2,1,0:T(8,128)S(1)} %dynamic-slice_maximum_fusion.2), channel_id=1, source_target_pairs={{0,16},{4,20},{8,24},{12,28},{16,0},{20,4},{24,8},{28,12},{32,48},... | collective-permute-start | bytes 393224 | tf_op jit(solution)/shard_map/ppermute | solution.py:28
  195.7 6.6 %collective-permute-start.15 = (f32[8,32,128]{2,1,0:T(8,128)S(1)}, f32[8,32,128]{2,1,0:T(8,128)S(1)}, u32[]{:S(2)}, u32[]{:S(2)}) collective-permute-start(f32[8,32,128]{2,1,0:T(8,128)S(1)} %max.63), channel_id=1, source_target_pairs={{0,128},{4,132},{8,136},{12,140},{16,144},{20,148},{24,152},{28,15... | collective-permute-start | bytes 393224 | tf_op jit(solution)/shard_map/ppermute | solution.py:28
  202.2 9.3 %collective-permute-start.16 = (f32[8,32,128]{2,1,0:T(8,128)S(1)}, f32[8,32,128]{2,1,0:T(8,128)S(1)}, u32[]{:S(2)}, u32[]{:S(2)}) collective-permute-start(f32[8,32,128]{2,1,0:T(8,128)S(1)} %max.64), channel_id=1, source_target_pairs={{0,32},{4,36},{8,40},{12,44},{16,48},{20,52},{24,56},{28,60},{32,0... | collective-permute-start | bytes 393224 | tf_op jit(solution)/shard_map/ppermute | solution.py:28
  212.8 1.3 collective-permute-start.24
  215.4 3.6 %collective-permute-start.25 = (f32[]{:T(128)}, f32[]{:T(128)}, u32[]{:S(2)}, u32[]{:S(2)}) collective-permute-start(f32[]{:T(128)} %add.204), channel_id=1, source_target_pairs={{0,8},{4,12},{8,0},{12,4},{16,24},{20,28},{24,16},{28,20},{32,40},... | collective-permute-start | bytes 20 | tf_op jit(solution)/shard_map/ppermute | solution.py:28
  219.7 3.6 %collective-permute-start.26 = (f32[]{:T(128)}, f32[]{:T(128)}, u32[]{:S(2)}, u32[]{:S(2)}) collective-permute-start(f32[]{:T(128)} %add.205), channel_id=1, source_target_pairs={{0,64},{4,68},{8,72},{12,76},{16,80},{20,84},{24,88},{28,92},{32,9... | collective-permute-start | bytes 20 | tf_op jit(solution)/shard_map/ppermute | solution.py:28
Sparse Core Ops, SparseCore 0:
  10.8 98.5 all-gather.1
